TPU v7x, 128 devices: a whole 4x4x4 slice. The times are simulated.
128 devices in a mesh: sector: 8 (over y, core), row: 16 (over x, z).
Axes of the slice: x: 4, y: 4, z: 4, core: 2. Of those that a mesh axis runs over, the one named last changes fastest.
Arguments:
- amplitudes: bfloat16 [8192, 4, 8192], P('sector', None, 'row'), may hold values from -6 to 6
- next_site: bfloat16 [8, 4, 8192, 2048], P('sector', None, 'row'), may hold values from -0.03125 to 0.03125
- sector_rows: int32 [8], replicated, may hold values from 512 to 1024, as said below
- moves: int32 [2, 8], replicated, may hold values from 0 to 128, as said below
- angles: float32 [2, 8, 128], replicated, may hold values from -3.140625 to 3.140625
- ranks: int32 [8], replicated, may hold values from 256 to 1024, as said below
Outputs:
- canonical: bfloat16 [2048, 8192], P('row', 'sector')
Inputs may be any that keep to these rules, and one draw needn't show every extreme that they name: `sector_rows`: one sector has exactly 1024 live rows and another exactly 512. `moves`: the entry of the last sector is 0, every other entry is 1 or more; for each gate some pair moves exactly 128 rows. `ranks`: each sector keeps at least half of its live rows and at most all of them; one sector keeps 1024 rows and one keeps 1024 // 4.
All inputs are finite; a program needn't handle non-finite values.
Results may differ from a plain program's by a relative error of at most 0.014.
Values may be sent and summed in bfloat16 or wider, within the bound.
No kernel may reach another device: no remote copies, remote signals or barrier semaphores. Data moves between devices by JAX's collectives and lax.ppermute only.
A program may use at most 128 MiB of HBM per device.

v0:
```python
import math

import jax
import jax.numpy as jnp
from jax import lax
from jax.sharding import PartitionSpec as P

KOUT = 2048


def shifted(x, axis, by):
    size = lax.axis_size(axis)
    pairs = [(i, i + by) for i in range(size) if 0 <= i + by < size]
    return lax.ppermute(x, axis, pairs)


def rotate_rows(
    padded, start_a, start_b, from_above, from_below, angle_here, angle_prev, count_here, count_prev
):
    slot_count = from_above.shape[0]
    slot_index = jnp.arange(slot_count)
    rows_a = lax.dynamic_slice_in_dim(padded, start_a, slot_count, 0)
    rows_b = lax.dynamic_slice_in_dim(padded, start_b, slot_count, 0)
    above_rows = from_above.astype(jnp.float32)
    below_rows = from_below.astype(jnp.float32)
    cos_here = jnp.cos(angle_here)[:, None, None]
    sin_here = jnp.sin(angle_here)[:, None, None]
    cos_prev = jnp.cos(angle_prev)[:, None, None]
    sin_prev = jnp.sin(angle_prev)[:, None, None]
    new_a = jnp.where(
        (slot_index < count_here)[:, None, None], cos_here * rows_a - sin_here * above_rows, rows_a
    )
    new_b = jnp.where(
        (slot_index < count_prev)[:, None, None], sin_prev * below_rows + cos_prev * rows_b, rows_b
    )
    padded = lax.dynamic_update_slice_in_dim(padded, new_a, start_a, 0)
    return lax.dynamic_update_slice_in_dim(padded, new_b, start_b, 0)


def per_device(amplitudes, next_site, sector_rows, moves, angles, ranks):
    sector_id = lax.axis_index("sector")
    sector_rows_count = amplitudes.shape[0]
    move_rows = sector_rows_count // 8
    row_index = jnp.arange(sector_rows_count)
    live_rows = sector_rows[sector_id]
    prev_id = jnp.maximum(sector_id - 1, 0)
    count_here = moves[:, sector_id]
    count_prev = jnp.where(sector_id > 0, moves[:, prev_id], 0)
    local_rows = jnp.where(
        (row_index < live_rows)[:, None, None], amplitudes.astype(jnp.float32), 0.0
    )
    tail_zeros = jnp.zeros((move_rows,) + local_rows.shape[1:], jnp.float32)
    padded = jnp.concatenate([local_rows, tail_zeros], 0)
    starts_a = [live_rows - count_here[0], live_rows - count_here[0] - count_here[1]]
    starts_b = [jnp.int32(0), count_prev[0]]
    for gate_index in range(2):
        send_up = lax.dynamic_slice_in_dim(padded, starts_a[gate_index], move_rows, 0).astype(
            jnp.bfloat16
        )
        send_down = lax.dynamic_slice_in_dim(padded, starts_b[gate_index], move_rows, 0).astype(
            jnp.bfloat16
        )
        from_below = shifted(send_up, "sector", 1)
        from_above = shifted(send_down, "sector", -1)
        padded = rotate_rows(
            padded,
            starts_a[gate_index],
            starts_b[gate_index],
            from_above,
            from_below,
            angles[gate_index][sector_id],
            angles[gate_index][prev_id],
            count_here[gate_index],
            count_prev[gate_index],
        )
    block_rows = padded[:sector_rows_count].astype(jnp.bfloat16)
    site_tensor = next_site[0]
    contracted = lax.psum_scatter(
        jnp.einsum("prk,lpr->kl", site_tensor, block_rows, preferred_element_type=jnp.float32),
        "row",
        scatter_dimension=0,
        tiled=True,
    ).astype(jnp.bfloat16)
    local_gram = lax.dot_general(
        contracted, contracted, (((0,), (0,)), ((), ())), preferred_element_type=jnp.float32
    )
    gram_matrix = lax.psum(local_gram, "row")
    dead_rows = (row_index >= live_rows).astype(jnp.float32)
    gram_matrix = gram_matrix + jnp.diag(dead_rows)
    factor_low = jnp.linalg.cholesky(gram_matrix)
    solved = jax.scipy.linalg.solve_triangular(
        factor_low, contracted.astype(jnp.float32).T, lower=True
    ).T
    kept_mask = ((row_index >= live_rows - ranks[sector_id]) & (row_index < live_rows)).astype(
        jnp.float32
    )
    return (solved * math.sqrt(KOUT) * kept_mask[None, :]).astype(jnp.bfloat16)


def solution(mesh):
    placed = (P("sector", None, "row"), P("sector", None, "row", None), P(), P(), P(), P())
    return jax.shard_map(
        per_device, mesh=mesh, in_specs=placed, out_specs=P("row", "sector"), check_vma=False
    )
```

profile of v0, /device:TPU:0, one launch (start us, length us, event | category | flops | bytes accessed | tf_op | source)
XLA Modules:
  0.0 639.9 jit_solution(2084765456773674766)
XLA Ops:
  11.0 3.8 convert_select_fusion
  25.2 8.1 %concatenate.30 = f32[1152,4,512]{2,0,1:T(8,128)} pad(f32[1024,4,512]{2,0,1:T(8,128)} %copy-done, f32[]{:T(128)} %constant.290.clone.1), padding=0_128x0_0x0_0 | pad | bytes 17825796 | tf_op jit(solution)/shard_map/concatenate | solution.py:53
  36.3 5.9 dynamic_update_slice.12
  47.8 3.8 collective-permute-start.3
  55.3 5.9 dynamic_update_slice.14
  61.2 5.9 dynamic_update_slice.15
  67.1 15.6 %fusion.2 = f32[2048,1024]{0,1:T(8,128)} fusion(bf16[1,4,512,2048]{3,2,1,0:T(8,128)(2,1)} %param.7, f32[1152,4,512]{2,0,1:T(8,128)} %dynamic_update_slice.15), kind=kOutput, calls=%fused_computation.7 | convolution fusion | flops 8589934592 | bytes 20971520 | tf_op jit(solution)/shard_map/prk,lpr->kl/dot_general | solution.py:79
  82.8 95.0 %reduce-scatter.2.cloned.1.call-done = f32[128,1024]{0,1:T(8,128)} async-done(((f32[2048,1024]{0,1:T(8,128)}), f32[128,1024]{0,1:T(8,128)}) %reduce-scatter.2.cloned.1.call-update) | async-done | bytes 524304 | tf_op jit(solution)/shard_map/reduce_scatter | solution.py:78
  177.7 3.9 fusion.46
  184.8 99.9 %all-reduce.4.cloned.1.call-done = f32[1024,1024]{0,1:T(8,128)} async-done(((f32[1024,1024]{0,1:T(8,128)}), f32[1024,1024]{0,1:T(8,128)}) %all-reduce.4.cloned.1.call-update) | async-done | bytes 4194320 | tf_op jit(solution)/shard_map/psum | solution.py:87
  284.7 4.8 select_add_fusion
  289.6 5.8 copy.9
  295.3 4.4 fusion.5
  301.7 11.7 %cholesky.222 = f32[128,128]{1,0:T(8,128)S(1)} custom-call(f32[128,128]{1,0:T(8,128)S(1)} %cholesky.577), custom_call_target="Cholesky" | custom-call | tf_op jit(solution)/shard_map/jit(cholesky)/cholesky | solution.py:90
  313.5 9.8 %custom-call.63 = f32[1,128,128]{1,2,0:T(8,128)S(1)} custom-call(f32[1,128,128]{2,1,0:T(8,128)S(1)} %get-tuple-element.73), custom_call_target="InvertDiagBlocksLowerTriangular" | custom-call | tf_op jit(solution)/shard_map/jit(cholesky)/cholesky | solution.py:90
  326.4 11.7 %cholesky.243 = f32[128,128]{1,0:T(8,128)S(1)} custom-call(f32[128,128]{1,0:T(8,128)S(1)} %cholesky.581), custom_call_target="Cholesky" | custom-call | tf_op jit(solution)/shard_map/jit(cholesky)/cholesky | solution.py:90
  341.2 9.8 %custom-call.64 = f32[1,128,128]{1,2,0:T(8,128)S(1)} custom-call(f32[1,128,128]{2,1,0:T(8,128)S(1)} %get-tuple-element.71), custom_call_target="InvertDiagBlocksLowerTriangular" | custom-call | tf_op jit(solution)/shard_map/jit(cholesky)/cholesky | solution.py:90
  356.5 11.7 %cholesky.466 = f32[128,128]{1,0:T(8,128)S(1)} custom-call(f32[128,128]{1,0:T(8,128)S(1)} %cholesky.586), custom_call_target="Cholesky" | custom-call | tf_op jit(solution)/shard_map/jit(cholesky)/cholesky | solution.py:90
  369.0 9.8 %custom-call.65 = f32[1,128,128]{1,2,0:T(8,128)S(1)} custom-call(f32[1,128,128]{2,1,0:T(8,128)S(1)} %get-tuple-element.69), custom_call_target="InvertDiagBlocksLowerTriangular" | custom-call | tf_op jit(solution)/shard_map/jit(cholesky)/cholesky | solution.py:90
  380.1 3.3 convolution_subtract_fusion.2
  383.4 11.7 %cholesky.485 = f32[128,128]{1,0:T(8,128)S(1)} custom-call(f32[128,128]{1,0:T(8,128)S(1)} %cholesky.591), custom_call_target="Cholesky" | custom-call | tf_op jit(solution)/shard_map/jit(cholesky)/cholesky | solution.py:90
  395.9 9.8 %custom-call.66 = f32[1,128,128]{1,2,0:T(8,128)S(1)} custom-call(f32[1,128,128]{2,1,0:T(8,128)S(1)} %get-tuple-element.67), custom_call_target="InvertDiagBlocksLowerTriangular" | custom-call | tf_op jit(solution)/shard_map/jit(cholesky)/cholesky | solution.py:90
  410.0 12.1 %cholesky.504 = f32[128,128]{1,0:T(8,128)S(1)} custom-call(f32[128,128]{1,0:T(8,128)S(1)} %cholesky.596), custom_call_target="Cholesky" | custom-call | tf_op jit(solution)/shard_map/jit(cholesky)/cholesky | solution.py:90
  422.9 9.8 %custom-call.67 = f32[1,128,128]{1,2,0:T(8,128)S(1)} custom-call(f32[1,128,128]{2,1,0:T(8,128)S(1)} %get-tuple-element.65), custom_call_target="InvertDiagBlocksLowerTriangular" | custom-call | tf_op jit(solution)/shard_map/jit(cholesky)/cholesky | solution.py:90
  436.9 11.7 %cholesky.524 = f32[128,128]{1,0:T(8,128)S(1)} custom-call(f32[128,128]{1,0:T(8,128)S(1)} %cholesky.601), custom_call_target="Cholesky" | custom-call | tf_op jit(solution)/shard_map/jit(cholesky)/cholesky | solution.py:90
  449.4 9.8 %custom-call.68 = f32[1,128,128]{1,2,0:T(8,128)S(1)} custom-call(f32[1,128,128]{2,1,0:T(8,128)S(1)} %get-tuple-element.63), custom_call_target="InvertDiagBlocksLowerTriangular" | custom-call | tf_op jit(solution)/shard_map/jit(cholesky)/cholesky | solution.py:90
  463.1 11.7 %cholesky.544 = f32[128,128]{1,0:T(8,128)S(1)} custom-call(f32[128,128]{1,0:T(8,128)S(1)} %cholesky.606), custom_call_target="Cholesky" | custom-call | tf_op jit(solution)/shard_map/jit(cholesky)/cholesky | solution.py:90
  475.6 9.8 %custom-call.69 = f32[1,128,128]{1,2,0:T(8,128)S(1)} custom-call(f32[1,128,128]{2,1,0:T(8,128)S(1)} %get-tuple-element.61), custom_call_target="InvertDiagBlocksLowerTriangular" | custom-call | tf_op jit(solution)/shard_map/jit(cholesky)/cholesky | solution.py:90
  488.4 11.7 %cholesky.562 = f32[128,128]{1,0:T(8,128)S(1)} custom-call(f32[128,128]{1,0:T(8,128)S(1)} %convolution_subtract_fusion.11), custom_call_target="Cholesky" | custom-call | tf_op jit(solution)/shard_map/jit(cholesky)/cholesky | solution.py:90
  511.2 4.8 select_select_fusion
  516.0 23.7 %while.1 = (s32[]{:T(128)}, f32[1024,1024]{0,1:T(8,128)}, s32[8,2]{0,1:T(2,128)S(1)}, f32[8,128,128]{2,1,0:T(8,128)S(1)}, s32[]{:T(128)}) while((s32[]{:T(128)}, f32[1024,1024]{0,1:T(8,128)}, s32[8,2]{0,1:T(2,128)S(1)}, f32[8,128,128]{2,1,0:T(8,128)S(1)}, s32[]{:T(128)}) %tuple.65), condition=%wide.while_cond, body=%wide.while_body.sunk | while | flops 2 | bytes 393321 | solution.py:91
  539.8 78.8 %custom-call.70 = f32[8,128,128]{1,2,0:T(8,128)S(1)} custom-call(f32[8,128,128]{2,1,0:T(8,128)S(1)} %get-tuple-element.12), custom_call_target="InvertDiagBlocksLowerTriangular" | custom-call | tf_op jit(solution)/shard_map/jit(_solve_triangular)/triangular_solve | solution.py:91
  (155 shorter events, 102.7 us)
Async XLA Ops:
  6.5 171.2 %reduce-scatter.2.cloned.1.call-start = ((), (), s32[]{:S(2)}) async-start(), calls=%async_computation.1 | async-start | bytes 8912896 | tf_op jit(solution)/shard_map/reduce_scatter | solution.py:78
  14.9 3.3 copy-start
  14.9 7.7 %copy-start.3 = (f32[2,8,128]{2,1,0:T(8,128)S(1)}, f32[2,8,128]{2,1,0:T(8,128)}, u32[]{:S(2)}) copy-start(f32[2,8,128]{2,1,0:T(8,128)} %param.10) | copy-start | bytes 24580
  18.2 16.5 %collective-permute-start = (bf16[128,4,512]{2,0,1:T(8,128)(2,1)S(1)}, bf16[128,4,512]{2,0,1:T(8,128)(2,1)S(1)}, u32[]{:S(2)}, u32[]{:S(2)}) collective-permute-start(bf16[128,4,512]{2,0,1:T(8,128)(2,1)S(1)} %get-tuple-element.34), channel_id=1, source_target_pairs={{16,0},{32,16},{48,32},{64,48},{80,64},{96,80},{112,96},{17,1},{33... | collective-permute-start | bytes 1572872 | tf_op jit(solution)/shard_map/ppermute | solution.py:14
  19.5 22.7 %collective-permute-start.1 = (bf16[128,4,512]{2,0,1:T(8,128)(2,1)S(1)}, bf16[128,4,512]{2,0,1:T(8,128)(2,1)S(1)}, u32[]{:S(2)}, u32[]{:S(2)}) collective-permute-start(bf16[128,4,512]{2,0,1:T(8,128)(2,1)S(1)} %get-tuple-element.33), channel_id=1, source_target_pairs={{0,16},{16,32},{32,48},{48,64},{64,80},{80,96},{96,112},{1,17},{17... | collective-permute-start | bytes 1572872 | tf_op jit(solution)/shard_map/ppermute | solution.py:14
  46.5 6.5 %collective-permute-start.2 = (bf16[128,4,512]{2,0,1:T(8,128)(2,1)S(1)}, bf16[128,4,512]{2,0,1:T(8,128)(2,1)S(1)}, u32[]{:S(2)}, u32[]{:S(2)}) collective-permute-start(bf16[128,4,512]{2,0,1:T(8,128)(2,1)S(1)} %get-tuple-element.32), channel_id=1, source_target_pairs={{16,0},{32,16},{48,32},{64,48},{80,64},{96,80},{112,96},{17,1},{33... | collective-permute-start | bytes 1572872 | tf_op jit(solution)/shard_map/ppermute | solution.py:14
  47.8 5.3 collective-permute-start.3
  82.7 99.0 %copy-start.4 = (s32[8]{0:T(128)S(1)}, s32[8]{0:T(128)}, u32[]{:S(2)}) copy-start(s32[8]{0:T(128)} %param.11) | copy-start | bytes 100
  82.7 202.0 %all-reduce.4.cloned.1.call-start = ((), (), s32[]{:S(2)}) async-start(), calls=%async_computation.2 | async-start | bytes 8388608 | tf_op jit(solution)/shard_map/psum | solution.py:87
  177.7 7.0 %copy-start.2 = (f32[128,1024]{0,1:T(8,128)S(1)}, f32[128,1024]{0,1:T(8,128)}, u32[]{:S(2)}) copy-start(f32[128,1024]{0,1:T(8,128)} %reduce-scatter.2.cloned.1.call-done) | copy-start | bytes 1572868
  299.8 1.9 copy-start.1
Sparse Core Ops, SparseCore 0:
  82.8 94.8 reduce-scatter.1
  181.8 102.8 all-reduce.3
where the time goes:
time: 650 us; the launch traced here: 640 us
  other arithmetic  277 us (43%)
  waiting for transfers between devices  195 us (30%)
  local copies, waits for them, and re-layouts  74.6 us (11%)
  matrix products  59.6 us (9%)
  between operations  24.2 us (4%)
  starting transfers between devices  9.49 us (1%)
    another operation x31, other arithmetic, per_device(): factor_low = jnp.linalg.cholesky(gram_matrix)  168 us
    psum x1, waiting for transfers between devices, per_device(): gram_matrix = lax.psum(local_gram, 'row')  99.9 us
    reduce_scatter x1, waiting for transfers between devices, per_device(): lax.psum_scatter(jnp.einsum('prk,lpr->kl', site_tensor, block_rows, prefe...  95 us
    another operation x3, other arithmetic, per_device(): jax.scipy.linalg.solve_triangular(factor_low, contracted.astype(jnp.float...  83.6 us
    another operation x14, matrix products, per_device(): factor_low = jnp.linalg.cholesky(gram_matrix)  27 us
    another operation x40, local copies, waits for them, and re-layouts  23.5 us
    dot_general x1, matrix products, per_device(): jnp.einsum('prk,lpr->kl', site_tensor, block_rows, preferred_element_type...  15.6 us
    another operation x15, matrix products, per_device(): jax.scipy.linalg.solve_triangular(factor_low, contracted.astype(jnp.float...  13.1 us
  transfers between devices with their start and end apart: 6, of which 3 were waited for; matrix products, arithmetic and copies ran while one was open for 3% of the time, Pallas kernels for 0%

commit v1 on v0

v1 whole, which is shorter than its diff:
```python
import math

import jax
import jax.numpy as jnp
from jax import lax
from jax.sharding import PartitionSpec as P

KOUT = 2048
BLOCK = 128
HI = lax.Precision.HIGHEST


def shifted(x, axis, by):
    size = lax.axis_size(axis)
    pairs = [(i, i + by) for i in range(size) if 0 <= i + by < size]
    return lax.ppermute(x, axis, pairs)


def rotated_window(own, partner, angle, count, sign):
    slot_index = jnp.arange(own.shape[0])
    own32 = own.astype(jnp.float32)
    partner32 = partner.astype(jnp.float32)
    cos_t = jnp.cos(angle)[:, None, None]
    sin_t = jnp.sin(angle)[:, None, None]
    if sign < 0:
        new = cos_t * own32 - sin_t * partner32
    else:
        new = sin_t * partner32 + cos_t * own32
    return jnp.where((slot_index < count)[:, None, None], new, own32).astype(jnp.bfloat16)


def dot(a, b):
    return jnp.dot(a, b, precision=HI, preferred_element_type=jnp.float32)


def cholesky_solve(gram, rhs):
    n = gram.shape[0]
    eye = jnp.eye(BLOCK, dtype=jnp.float32)
    trailing = gram
    rest = rhs
    solved = []
    for start in range(0, n, BLOCK):
        diag = trailing[:BLOCK, :BLOCK]
        factor = jnp.linalg.cholesky(diag)
        inverse = lax.linalg.triangular_solve(factor, eye, left_side=True, lower=True)
        head = dot(inverse, rest[:BLOCK])
        solved.append(head)
        if start + BLOCK < n:
            panel = lax.dot_general(
                trailing[BLOCK:, :BLOCK], inverse, (((1,), (1,)), ((), ())),
                precision=HI, preferred_element_type=jnp.float32,
            )
            trailing = trailing[BLOCK:, BLOCK:] - lax.dot_general(
                panel, panel, (((1,), (1,)), ((), ())),
                precision=HI, preferred_element_type=jnp.float32,
            )
            rest = rest[BLOCK:] - dot(panel, head)
    return jnp.concatenate(solved, 0)


def per_device(amplitudes, next_site, sector_rows, moves, angles, ranks):
    sector_id = lax.axis_index("sector")
    rows = amplitudes.shape[0]
    move_rows = angles.shape[-1]
    row_index = jnp.arange(rows)
    live_rows = sector_rows[sector_id]
    prev_id = jnp.maximum(sector_id - 1, 0)
    count_here = moves[:, sector_id]
    count_prev = jnp.where(sector_id > 0, moves[:, prev_id], 0)
    masked = jnp.where((row_index < live_rows)[:, None, None], amplitudes, jnp.zeros((), amplitudes.dtype))
    padded = jnp.concatenate(
        [masked, jnp.zeros((move_rows,) + masked.shape[1:], masked.dtype)], 0
    )
    starts_a = [live_rows - count_here[0], live_rows - count_here[0] - count_here[1]]
    starts_b = [jnp.int32(0), count_prev[0]]
    own_a = [lax.dynamic_slice_in_dim(padded, s, move_rows, 0) for s in starts_a]
    own_b = [lax.dynamic_slice_in_dim(padded, s, move_rows, 0) for s in starts_b]
    from_below = [shifted(w, "sector", 1) for w in own_a]
    from_above = [shifted(w, "sector", -1) for w in own_b]
    new_a = [
        rotated_window(own_a[g], from_above[g], angles[g][sector_id], count_here[g], -1)
        for g in range(2)
    ]
    new_b = [
        rotated_window(own_b[g], from_below[g], angles[g][prev_id], count_prev[g], 1)
        for g in range(2)
    ]
    padded = lax.dynamic_update_slice_in_dim(padded, new_a[1], starts_a[1], 0)
    padded = lax.dynamic_update_slice_in_dim(padded, new_a[0], starts_a[0], 0)
    padded = lax.dynamic_update_slice_in_dim(padded, new_b[0], starts_b[0], 0)
    padded = lax.dynamic_update_slice_in_dim(padded, new_b[1], starts_b[1], 0)
    block_rows = padded[:rows]
    site_tensor = next_site[0]
    contracted = lax.psum_scatter(
        jnp.einsum("prk,lpr->kl", site_tensor, block_rows, preferred_element_type=jnp.float32),
        "row",
        scatter_dimension=0,
        tiled=True,
    ).astype(jnp.bfloat16)
    gathered = lax.all_gather(contracted, "row", axis=0, tiled=True)
    gram_matrix = lax.dot_general(
        gathered, gathered, (((0,), (0,)), ((), ())), preferred_element_type=jnp.float32
    )
    dead_rows = (row_index >= live_rows).astype(jnp.float32)
    gram_matrix = gram_matrix + jnp.diag(dead_rows)
    solved = cholesky_solve(gram_matrix, contracted.astype(jnp.float32).T).T
    kept_mask = ((row_index >= live_rows - ranks[sector_id]) & (row_index < live_rows)).astype(
        jnp.float32
    )
    return (solved * math.sqrt(KOUT) * kept_mask[None, :]).astype(jnp.bfloat16)


def solution(mesh):
    placed = (P("sector", None, "row"), P("sector", None, "row", None), P(), P(), P(), P())
    return jax.shard_map(
        per_device, mesh=mesh, in_specs=placed, out_specs=P("row", "sector"), check_vma=False
    )
```

time: 650 us -> 478 us (0.74)
  other arithmetic: 277 us -> 208 us
  waiting for transfers between devices: 195 us -> 145 us
  local copies, waits for them, and re-layouts: 74.6 us -> 33.8 us
  matrix products: 59.6 us -> 51.8 us
    psum x1 -> x0, waiting for transfers between devices: 99.9 us -> none  [per_device(): gram_matrix = lax.psum(local_gram, 'row')]
    another operation x34 -> x40, other arithmetic: 252 us -> 186 us  [the longest x24 101 us: cholesky_solve(): factor = jnp.linalg.cholesky(diag)]
    all_gather x0 -> x1, waiting for transfers between devices: none -> 53.2 us  [per_device(): gathered = lax.all_gather(contracted, 'row', axis=0, tiled=True)]
    another operation x29 -> x8, matrix products: 40 us -> 2.28 us  [cholesky_solve(): lax.linalg.triangular_solve(factor, eye, left_side=True, lower=True)]
    another operation x66 -> x0, local copies, waits for them, and re-layouts: 32.4 us -> none
    dot_general x1 -> x30, matrix products: 3.93 us -> 35.1 us  [the longest x7 12.9 us: cholesky_solve(): lax.dot_general(panel, panel, (((1,), (1,)), ((), ())), precision=HI, pre...]
  transfers between devices with their start and end apart: 6 -> 6, of which waited for: 3 -> 2; matrix products, arithmetic and copies ran while one was open for 3% -> 4% of each run, Pallas kernels for 0% -> 0%
where the time goes in v1:
time: 478 us; the launch traced here: 470 us
  other arithmetic  208 us (44%)
  waiting for transfers between devices  145 us (30%)
  matrix products  51.8 us (11%)
  local copies, waits for them, and re-layouts  33.8 us (7%)
  between operations  19.8 us (4%)
  starting transfers between devices  11.8 us (2%)
    another operation x24, other arithmetic, cholesky_solve(): factor = jnp.linalg.cholesky(diag)  101 us
    reduce_scatter x1, waiting for transfers between devices, per_device(): lax.psum_scatter(jnp.einsum('prk,lpr->kl', site_tensor, block_rows, prefe...  91.3 us
    another operation x16, other arithmetic, cholesky_solve(): lax.linalg.triangular_solve(factor, eye, left_side=True, lower=True)  85.5 us
    all_gather x1, waiting for transfers between devices, per_device(): gathered = lax.all_gather(contracted, 'row', axis=0, tiled=True)  53.2 us
    dot_general x1, matrix products, per_device(): jnp.einsum('prk,lpr->kl', site_tensor, block_rows, preferred_element_type...  14.4 us
    dot_general x7, matrix products, cholesky_solve(): lax.dot_general(panel, panel, (((1,), (1,)), ((), ())), precision=HI, pre...  12.9 us
    ppermute x4, starting transfers between devices, shifted(): return lax.ppermute(x, axis, pairs)  11.8 us
  transfers between devices with their start and end apart: 6, of which 2 were waited for; matrix products, arithmetic and copies ran while one was open for 4% of the time, Pallas kernels for 0%

profile of v1, /device:TPU:0, one launch (start us, length us, event | category | flops | bytes accessed | tf_op | source)
XLA Modules:
  0.0 469.6 jit_solution(3784771538041529058)
XLA Ops:
  11.8 5.1 %copy_select_fusion = bf16[1024,4,512]{2,0,1:T(8,128)(2,1)S(1)} fusion(bf16[1024,4,512]{2,1,0:T(4,128)(2,1)} %param.9, pred[1024]{0:T(1024)(128)(4,1)S(1)} %iota_compare_fusion.13), kind=kLoop, calls=%fused_computation.4 | loop fusion | flops 2097152 | bytes 8389632 | tf_op jit(solution)/shard_map/jit(_where)/select_n | solution.py:70
  20.3 3.1 collective-permute-start.3
  27.2 2.0 fusion.9
  30.4 6.1 %collective-permute-start.2 = (bf16[128,4,512]{2,0,1:T(8,128)(2,1)S(1)}, bf16[128,4,512]{2,0,1:T(8,128)(2,1)S(1)}, u32[]{:S(2)}, u32[]{:S(2)}) collective-permute-start(bf16[128,4,512]{2,0,1:T(8,128)(2,1)S(1)} %get-tuple-element.10), channel_id=1, source_target_pairs={{0,16},{16,32},{32,48},{48,64},{64,80},{80,96},{96,112},{1,17},{17... | collective-permute-start | bytes 1572872 | tf_op jit(solution)/shard_map/ppermute | solution.py:16
  36.6 2.5 concatenate.6
  40.7 5.6 %dynamic_update_slice.12 = bf16[1152,4,512]{2,0,1:T(8,128)(2,1)} dynamic-update-slice(bf16[1152,4,512]{2,0,1:T(8,128)(2,1)} %concatenate.6, bf16[128,4,512]{2,0,1:T(8,128)(2,1)S(1)} %fusion.7, s32[]{:T(128)S(6)} %select_n.58, s32[]{:T(128)} %constant.51.clone.1, s32[]{:T(128)} %constant.51.clone.1) | dynamic-update-slice | bytes 1048580 | tf_op jit(solution)/shard_map/dynamic_update_slice | solution.py:88
  46.3 5.5 %dynamic_update_slice.13 = bf16[1152,4,512]{2,0,1:T(8,128)(2,1)} dynamic-update-slice(bf16[1152,4,512]{2,0,1:T(8,128)(2,1)} %dynamic_update_slice.12, bf16[128,4,512]{2,0,1:T(8,128)(2,1)S(1)} %get-tuple-element.9, s32[]{:T(128)S(6)} %select_n.63, s32[]{:T(128)} %constant.51.clone.1, s32[]{:T(128)} %constant.51.clone.1) | dynamic-update-slice | bytes 1048580 | tf_op jit(solution)/shard_map/dynamic_update_slice | solution.py:89
  51.8 2.2 fusion.14
  54.0 5.5 %dynamic_update_slice.15 = bf16[1152,4,512]{2,0,1:T(8,128)(2,1)} dynamic-update-slice(bf16[1152,4,512]{2,0,1:T(8,128)(2,1)} %fusion.14, bf16[128,4,512]{2,0,1:T(8,128)(2,1)S(1)} %get-tuple-element.11, s32[]{:T(128)S(6)} %select_n.61, s32[]{:T(128)} %constant.51.clone.1, s32[]{:T(128)} %constant.51.clone.1) | dynamic-update-slice | bytes 1048580 | tf_op jit(solution)/shard_map/dynamic_update_slice | solution.py:91
  59.5 14.4 %fusion.2 = f32[2048,1024]{0,1:T(8,128)} fusion(bf16[1,4,512,2048]{3,2,1,0:T(8,128)(2,1)} %param.10, bf16[1152,4,512]{2,0,1:T(8,128)(2,1)} %dynamic_update_slice.15), kind=kOutput, calls=%fused_computation.2 | convolution fusion | flops 8589934592 | bytes 20971520 | tf_op jit(solution)/shard_map/prk,lpr->kl/dot_general | solution.py:95
  74.0 91.3 %reduce-scatter.2.cloned.1.call-done = f32[128,1024]{0,1:T(8,128)} async-done(((f32[2048,1024]{0,1:T(8,128)}), f32[128,1024]{0,1:T(8,128)}) %reduce-scatter.2.cloned.1.call-update) | async-done | bytes 524304 | tf_op jit(solution)/shard_map/reduce_scatter | solution.py:94
  171.3 53.2 %all-gather.2.cloned.1.call-done = bf16[2048,1024]{0,1:T(8,128)(2,1)} async-done(((bf16[128,1024]{0,1:T(8,128)(2,1)}), bf16[2048,1024]{0,1:T(8,128)(2,1)}) %all-gather.2.cloned.1.call-update) | async-done | bytes 4194320 | tf_op jit(solution)/shard_map/all_gather | solution.py:100
  224.5 8.3 %select_add_fusion = f32[1024,1024]{0,1:T(8,128)S(1)} fusion(f32[1024]{0:T(1024)S(1)} %fusion.84, bf16[2048,1024]{0,1:T(8,128)(2,1)} %all-gather.2.cloned.1.call-done), kind=kOutput, calls=%fused_computation.5 | convolution fusion | flops 4298113024 | bytes 8392704 | tf_op jit(solution)/shard_map/dot_general | solution.py:101
  235.7 11.7 %cholesky.134 = f32[128,128]{1,0:T(8,128)S(1)} custom-call(f32[128,128]{1,0:T(8,128)S(1)} %fusion.81), custom_call_target="Cholesky" | custom-call | tf_op jit(solution)/shard_map/jit(cholesky)/cholesky | solution.py:44
  248.7 9.8 %custom-call.12 = f32[1,128,128]{1,2,0:T(8,128)S(1)} custom-call(f32[1,128,128]{2,1,0:T(8,128)S(1)} %fusion.44), custom_call_target="InvertDiagBlocksLowerTriangular" | custom-call | tf_op jit(solution)/shard_map/triangular_solve/custom-call.0 | solution.py:45
  262.2 4.6 slice_subtract_fusion
  269.0 12.7 %cholesky.145 = f32[128,128]{1,0:T(8,128)S(1)} custom-call(f32[128,128]{1,0:T(8,128)} %fusion.79), custom_call_target="Cholesky" | custom-call | tf_op jit(solution)/shard_map/jit(cholesky)/cholesky | solution.py:44
  283.7 10.6 %custom-call.13 = f32[1,128,128]{1,2,0:T(8,128)S(1)} custom-call(f32[1,128,128]{2,1,0:T(8,128)} %fusion.45), custom_call_target="InvertDiagBlocksLowerTriangular" | custom-call | tf_op jit(solution)/shard_map/triangular_solve/custom-call.0 | solution.py:45
  296.0 2.0 slice_subtract_fusion.1
  300.4 11.7 %cholesky.156 = f32[128,128]{1,0:T(8,128)S(1)} custom-call(f32[128,128]{1,0:T(8,128)S(1)} %fusion.77), custom_call_target="Cholesky" | custom-call | tf_op jit(solution)/shard_map/jit(cholesky)/cholesky | solution.py:44
  313.5 10.2 %custom-call.14 = f32[1,128,128]{1,2,0:T(8,128)S(1)} custom-call(f32[1,128,128]{2,1,0:T(8,128)S(1)} %fusion.46), custom_call_target="InvertDiagBlocksLowerTriangular" | custom-call | tf_op jit(solution)/shard_map/triangular_solve/custom-call.0 | solution.py:45
  325.7 2.9 slice_subtract_fusion.2
  328.7 11.7 %cholesky.167 = f32[128,128]{1,0:T(8,128)S(1)} custom-call(f32[128,128]{1,0:T(8,128)S(1)} %fusion.75), custom_call_target="Cholesky" | custom-call | tf_op jit(solution)/shard_map/jit(cholesky)/cholesky | solution.py:44
  341.9 9.8 %custom-call.15 = f32[1,128,128]{1,2,0:T(8,128)S(1)} custom-call(f32[1,128,128]{2,1,0:T(8,128)S(1)} %fusion.47), custom_call_target="InvertDiagBlocksLowerTriangular" | custom-call | tf_op jit(solution)/shard_map/triangular_solve/custom-call.0 | solution.py:45
  355.6 11.9 %cholesky.178 = f32[128,128]{1,0:T(8,128)S(1)} custom-call(f32[128,128]{1,0:T(8,128)S(1)} %fusion.73), custom_call_target="Cholesky" | custom-call | tf_op jit(solution)/shard_map/jit(cholesky)/cholesky | solution.py:44
  368.9 9.8 %custom-call.16 = f32[1,128,128]{1,2,0:T(8,128)S(1)} custom-call(f32[1,128,128]{2,1,0:T(8,128)S(1)} %fusion.48), custom_call_target="InvertDiagBlocksLowerTriangular" | custom-call | tf_op jit(solution)/shard_map/triangular_solve/custom-call.0 | solution.py:45
  382.3 11.7 %cholesky.189 = f32[128,128]{1,0:T(8,128)S(1)} custom-call(f32[128,128]{1,0:T(8,128)S(1)} %fusion.71), custom_call_target="Cholesky" | custom-call | tf_op jit(solution)/shard_map/jit(cholesky)/cholesky | solution.py:44
  395.5 9.8 %custom-call.17 = f32[1,128,128]{1,2,0:T(8,128)S(1)} custom-call(f32[1,128,128]{2,1,0:T(8,128)S(1)} %fusion.49), custom_call_target="InvertDiagBlocksLowerTriangular" | custom-call | tf_op jit(solution)/shard_map/triangular_solve/custom-call.0 | solution.py:45
  407.3 11.7 %cholesky.200 = f32[128,128]{1,0:T(8,128)S(1)} custom-call(f32[128,128]{1,0:T(8,128)S(1)} %fusion.69), custom_call_target="Cholesky" | custom-call | tf_op jit(solution)/shard_map/jit(cholesky)/cholesky | solution.py:44
  420.2 9.8 %custom-call.18 = f32[1,128,128]{1,2,0:T(8,128)S(1)} custom-call(f32[1,128,128]{2,1,0:T(8,128)S(1)} %fusion.50), custom_call_target="InvertDiagBlocksLowerTriangular" | custom-call | tf_op jit(solution)/shard_map/triangular_solve/custom-call.0 | solution.py:45
  437.6 12.0 %cholesky.211 = f32[128,128]{1,0:T(8,128)S(1)} custom-call(f32[128,128]{1,0:T(8,128)S(1)} %fusion.67), custom_call_target="Cholesky" | custom-call | tf_op jit(solution)/shard_map/jit(cholesky)/cholesky | solution.py:44
  450.9 9.8 %custom-call.19 = f32[1,128,128]{1,2,0:T(8,128)S(1)} custom-call(f32[1,128,128]{2,1,0:T(8,128)S(1)} %fusion.51), custom_call_target="InvertDiagBlocksLowerTriangular" | custom-call | tf_op jit(solution)/shard_map/triangular_solve/custom-call.0 | solution.py:45
  (142 shorter events, 60.6 us)
Async XLA Ops:
  6.5 158.8 %reduce-scatter.2.cloned.1.call-start = ((), (), s32[]{:S(2)}) async-start(), calls=%async_computation.1 | async-start | bytes 8912896 | tf_op jit(solution)/shard_map/reduce_scatter | solution.py:94
  16.9 1.9 copy-start
  18.8 8.2 %copy-start.14 = (f32[2,8,128]{2,1,0:T(8,128)S(1)}, f32[2,8,128]{2,1,0:T(8,128)}, u32[]{:S(2)}) copy-start(f32[2,8,128]{2,1,0:T(8,128)} %param.13) | copy-start | bytes 24580
  19.0 8.1 %collective-permute-start.1 = (bf16[128,4,512]{2,0,1:T(8,128)(2,1)S(1)}, bf16[128,4,512]{2,0,1:T(8,128)(2,1)S(1)}, u32[]{:S(2)}, u32[]{:S(2)}) collective-permute-start(bf16[128,4,512]{2,0,1:T(8,128)(2,1)S(1)} %get-tuple-element.13), channel_id=1, source_target_pairs={{16,0},{32,16},{48,32},{64,48},{80,64},{96,80},{112,96},{17,1},{33... | collective-permute-start | bytes 1572872 | tf_op jit(solution)/shard_map/ppermute | solution.py:16
  20.3 6.8 %collective-permute-start.3 = (bf16[128,4,512]{2,0,1:T(8,128)(2,1)S(1)}, bf16[128,4,512]{2,0,1:T(8,128)(2,1)S(1)}, u32[]{:S(2)}, u32[]{:S(2)}) collective-permute-start(bf16[128,4,512]{2,0,1:T(8,128)(2,1)S(1)} %get-tuple-element.14), channel_id=1, source_target_pairs={{0,16},{16,32},{32,48},{48,64},{64,80},{80,96},{96,112},{1,17},{17... | collective-permute-start | bytes 1572872 | tf_op jit(solution)/shard_map/ppermute | solution.py:16
  25.4 11.2 %copy-start.1 = (bf16[1024,4,512]{2,0,1:T(8,128)(2,1)S(1)}, bf16[1024,4,512]{2,0,1:T(8,128)(2,1)}, u32[]{:S(2)}) copy-start(bf16[1024,4,512]{2,0,1:T(8,128)(2,1)} %copy-done) | copy-start | bytes 12582916
  29.1 11.3 %collective-permute-start = (bf16[128,4,512]{2,0,1:T(8,128)(2,1)S(1)}, bf16[128,4,512]{2,0,1:T(8,128)(2,1)S(1)}, u32[]{:S(2)}, u32[]{:S(2)}) collective-permute-start(bf16[128,4,512]{2,0,1:T(8,128)(2,1)S(1)} %get-tuple-element.12), channel_id=1, source_target_pairs={{16,0},{32,16},{48,32},{64,48},{80,64},{96,80},{112,96},{17,1},{33... | collective-permute-start | bytes 1572872 | tf_op jit(solution)/shard_map/ppermute | solution.py:16
  30.4 21.4 %collective-permute-start.2 = (bf16[128,4,512]{2,0,1:T(8,128)(2,1)S(1)}, bf16[128,4,512]{2,0,1:T(8,128)(2,1)S(1)}, u32[]{:S(2)}, u32[]{:S(2)}) collective-permute-start(bf16[128,4,512]{2,0,1:T(8,128)(2,1)S(1)} %get-tuple-element.10), channel_id=1, source_target_pairs={{0,16},{16,32},{32,48},{48,64},{64,80},{80,96},{96,112},{1,17},{17... | collective-permute-start | bytes 1572872 | tf_op jit(solution)/shard_map/ppermute | solution.py:16
  74.0 93.2 %copy-start.15 = (s32[8]{0:T(128)S(1)}, s32[8]{0:T(128)}, u32[]{:S(2)}) copy-start(s32[8]{0:T(128)} %param.14) | copy-start | bytes 100
  74.0 150.5 %all-gather.2.cloned.1.call-start = ((), (), s32[]{:S(2)}) async-start(), calls=%async_computation.2 | async-start | bytes 4456448 | tf_op jit(solution)/shard_map/all_gather | solution.py:100
  232.8 1.9 copy-start.8
  258.9 0.6 copy-start.13
  261.4 0.8 copy-start.3
  294.6 0.6 copy-start.11
  296.0 2.1 copy-start.5
  298.1 1.4 copy-start.2
  324.0 27.7 %copy-start.12 = (f32[128,128]{1,0:T(8,128)}, f32[128,128]{1,0:T(8,128)S(1)}, u32[]{:S(2)}) copy-start(f32[128,128]{1,0:T(8,128)S(1)} %fusion.34) | copy-start | bytes 196612
  352.6 79.1 %copy-start.4 = (f32[896,128]{1,0:T(8,128)S(1)}, f32[896,128]{1,0:T(8,128)}, u32[]{:S(2)}) copy-start(f32[896,128]{1,0:T(8,128)} %copy-done.3) | copy-start | bytes 1376260
  353.6 1.0 copy-start.7
  354.6 78.6 %copy-start.6 = (f32[768,128]{1,0:T(8,128)S(1)}, f32[768,128]{1,0:T(8,128)}, u32[]{:S(2)}) copy-start(f32[768,128]{1,0:T(8,128)} %copy-done.5) | copy-start | bytes 1179652
  405.6 0.6 copy-start.9
  407.1 29.2 %copy-start.10 = (f32[128,128]{1,0:T(8,128)S(1)}, f32[128,128]{1,0:T(8,128)}, u32[]{:S(2)}) copy-start(f32[128,128]{1,0:T(8,128)} %copy-done.9) | copy-start | bytes 196612
Sparse Core Ops, SparseCore 0:
  74.1 91.2 reduce-scatter.1
  167.5 56.9 all-gather.1

commit v2 on v1

--- a/solution.py
+++ b/solution.py
@@ -3,6 +3,7 @@
 import jax
 import jax.numpy as jnp
 from jax import lax
+from jax.experimental import pallas as pl
 from jax.sharding import PartitionSpec as P
 
 KOUT = 2048
@@ -33,16 +34,50 @@
     return jnp.dot(a, b, precision=HI, preferred_element_type=jnp.float32)
 
 
+def factor_inverse_kernel(d_ref, o_ref):
+    n = d_ref.shape[0]
+    lane = lax.broadcasted_iota(jnp.int32, (n, n), 1)
+    sub = lax.broadcasted_iota(jnp.int32, (n, n), 0)
+    lane_row = lax.broadcasted_iota(jnp.int32, (1, n), 1)
+    sub_col = lax.broadcasted_iota(jnp.int32, (n, 1), 0)
+
+    def body(j, carry):
+        a, w = carry
+        col = jnp.sum(jnp.where(lane == j, a, 0.0), axis=1, keepdims=True)
+        row = jnp.sum(jnp.where(sub == j, a, 0.0), axis=0, keepdims=True)
+        piv = jnp.sum(jnp.where(lane_row == j, row, 0.0), axis=1, keepdims=True)
+        r = lax.rsqrt(piv)
+        lcol = jnp.where(sub_col >= j, col * r, 0.0)
+        lrow = jnp.where(lane_row >= j, row * r, 0.0)
+        a = a - lcol * lrow
+        wj = jnp.sum(jnp.where(sub == j, w, 0.0), axis=0, keepdims=True) * r
+        w = jnp.where(sub == j, wj, w - lcol * wj)
+        return a, w
+
+    w0 = (sub == lane).astype(jnp.float32)
+    _, w = lax.fori_loop(0, n, body, (d_ref[...], w0))
+    o_ref[...] = w
+
+
+def factor_inverse(diag):
+    n = diag.shape[0]
+    return pl.pallas_call(
+        factor_inverse_kernel,
+        out_shape=jax.ShapeDtypeStruct((n, n), jnp.float32),
+        cost_estimate=pl.CostEstimate(
+            flops=6 * n * n * n, transcendentals=n, bytes_accessed=8 * n * n
+        ),
+    )(diag)
+
+
 def cholesky_solve(gram, rhs):
     n = gram.shape[0]
-    eye = jnp.eye(BLOCK, dtype=jnp.float32)
     trailing = gram
     rest = rhs
     solved = []
     for start in range(0, n, BLOCK):
         diag = trailing[:BLOCK, :BLOCK]
-        factor = jnp.linalg.cholesky(diag)
-        inverse = lax.linalg.triangular_solve(factor, eye, left_side=True, lower=True)
+        inverse = factor_inverse(diag)
         head = dot(inverse, rest[:BLOCK])
         solved.append(head)
         if start + BLOCK < n:

time: 478 us -> 425 us (0.89); the launches traced: 470 us -> 424 us
  other arithmetic: 208 us -> 18.1 us
  Pallas kernels: 0 us -> 146 us
    another operation x40 -> x0, other arithmetic: 186 us -> none  [the longest x24 101 us: cholesky_solve(): factor = jnp.linalg.cholesky(diag)]
    pallas_call x0 -> x8, Pallas kernels: none -> 146 us  [factor_inverse(): pl.pallas_call(factor_inverse_kernel, out_shape=jax.ShapeDtypeStruct((n,...]
  transfers between devices with their start and end apart: 6 -> 6, of which waited for: 2 -> 2; matrix products, arithmetic and copies ran while one was open for 4% -> 5% of each run, Pallas kernels for 0% -> 0%
where the time goes in v2:
time: 425 us; the launch traced here: 424 us
  Pallas kernels  146 us (34%)
  waiting for transfers between devices  144 us (34%)
  matrix products  50.3 us (12%)
  local copies, waits for them, and re-layouts  34.4 us (8%)
  between operations  19 us (4%)
  other arithmetic  18.1 us (4%)
  starting transfers between devices  11.9 us (3%)
    pallas_call x8, Pallas kernels, factor_inverse(): pl.pallas_call(factor_inverse_kernel, out_shape=jax.ShapeDtypeStruct((n,...  146 us
    reduce_scatter x1, waiting for transfers between devices, per_device(): lax.psum_scatter(jnp.einsum('prk,lpr->kl', site_tensor, block_rows, prefe...  90.8 us
    all_gather x1, waiting for transfers between devices, per_device(): gathered = lax.all_gather(contracted, 'row', axis=0, tiled=True)  53.3 us
    dot_general x1, matrix products, per_device(): jnp.einsum('prk,lpr->kl', site_tensor, block_rows, preferred_element_type...  14.6 us
    dot_general x7, matrix products, cholesky_solve(): lax.dot_general(panel, panel, (((1,), (1,)), ((), ())), precision=HI, pre...  13.5 us
    ppermute x4, starting transfers between devices, shifted(): return lax.ppermute(x, axis, pairs)  11.7 us
    dot_general x7, matrix products, cholesky_solve(): lax.dot_general(trailing[BLOCK:, :BLOCK], inverse, (((1,), (1,)), ((), ()...  9.1 us
  transfers between devices with their start and end apart: 6, of which 2 were waited for; matrix products, arithmetic and copies ran while one was open for 5% of the time, Pallas kernels for 0%

profile of v2, /device:TPU:0, one launch (start us, length us, event | category | flops | bytes accessed | tf_op | source)
XLA Modules:
  0.0 423.8 jit_solution(10114590815498034272)
XLA Ops:
  11.6 5.1 %copy_select_fusion = bf16[1024,4,512]{2,0,1:T(8,128)(2,1)S(1)} fusion(bf16[1024,4,512]{2,1,0:T(4,128)(2,1)} %param.6, pred[1024]{0:T(1024)(128)(4,1)S(1)} %iota_compare_fusion.3), kind=kLoop, calls=%fused_computation.4 | loop fusion | flops 2097152 | bytes 8389632 | tf_op jit(solution)/shard_map/jit(_where)/select_n | solution.py:105
  16.7 2.0 copy-done
  20.2 3.1 collective-permute-start.3
  27.1 2.0 fusion.9
  30.4 6.1 %collective-permute-start.2 = (bf16[128,4,512]{2,0,1:T(8,128)(2,1)S(1)}, bf16[128,4,512]{2,0,1:T(8,128)(2,1)S(1)}, u32[]{:S(2)}, u32[]{:S(2)}) collective-permute-start(bf16[128,4,512]{2,0,1:T(8,128)(2,1)S(1)} %get-tuple-element.8), channel_id=1, source_target_pairs={{0,16},{16,32},{32,48},{48,64},{64,80},{80,96},{96,112},{1,17},{17... | collective-permute-start | bytes 1572872 | tf_op jit(solution)/shard_map/ppermute | solution.py:17
  36.4 2.6 concatenate.6
  40.6 5.6 %dynamic_update_slice.12 = bf16[1152,4,512]{2,0,1:T(8,128)(2,1)} dynamic-update-slice(bf16[1152,4,512]{2,0,1:T(8,128)(2,1)} %concatenate.6, bf16[128,4,512]{2,0,1:T(8,128)(2,1)S(1)} %fusion.7, s32[]{:T(128)S(6)} %select_n.55, s32[]{:T(128)} %constant.22.clone.1, s32[]{:T(128)} %constant.22.clone.1) | dynamic-update-slice | bytes 1048580 | tf_op jit(solution)/shard_map/dynamic_update_slice | solution.py:123
  46.2 5.6 %dynamic_update_slice.13 = bf16[1152,4,512]{2,0,1:T(8,128)(2,1)} dynamic-update-slice(bf16[1152,4,512]{2,0,1:T(8,128)(2,1)} %dynamic_update_slice.12, bf16[128,4,512]{2,0,1:T(8,128)(2,1)S(1)} %get-tuple-element.7, s32[]{:T(128)S(6)} %select_n.60, s32[]{:T(128)} %constant.22.clone.1, s32[]{:T(128)} %constant.22.clone.1) | dynamic-update-slice | bytes 1048580 | tf_op jit(solution)/shard_map/dynamic_update_slice | solution.py:124
  51.8 2.2 fusion.14
  53.9 5.6 %dynamic_update_slice.15 = bf16[1152,4,512]{2,0,1:T(8,128)(2,1)} dynamic-update-slice(bf16[1152,4,512]{2,0,1:T(8,128)(2,1)} %fusion.14, bf16[128,4,512]{2,0,1:T(8,128)(2,1)S(1)} %get-tuple-element.9, s32[]{:T(128)S(6)} %select_n.58, s32[]{:T(128)} %constant.22.clone.1, s32[]{:T(128)} %constant.22.clone.1) | dynamic-update-slice | bytes 1048580 | tf_op jit(solution)/shard_map/dynamic_update_slice | solution.py:126
  59.5 14.6 %fusion.2 = f32[2048,1024]{0,1:T(8,128)} fusion(bf16[1,4,512,2048]{3,2,1,0:T(8,128)(2,1)} %param.7, bf16[1152,4,512]{2,0,1:T(8,128)(2,1)} %dynamic_update_slice.15), kind=kOutput, calls=%fused_computation.2 | convolution fusion | flops 8589934592 | bytes 20971520 | tf_op jit(solution)/shard_map/prk,lpr->kl/dot_general | solution.py:130
  74.3 90.8 %reduce-scatter.2.cloned.1.call-done = f32[128,1024]{0,1:T(8,128)} async-done(((f32[2048,1024]{0,1:T(8,128)}), f32[128,1024]{0,1:T(8,128)}) %reduce-scatter.2.cloned.1.call-update) | async-done | bytes 524304 | tf_op jit(solution)/shard_map/reduce_scatter | solution.py:129
  165.1 1.8 convert_element_type.70
  170.9 53.3 %all-gather.2.cloned.1.call-done = bf16[2048,1024]{0,1:T(8,128)(2,1)} async-done(((bf16[128,1024]{0,1:T(8,128)(2,1)}), bf16[2048,1024]{0,1:T(8,128)(2,1)}) %all-gather.2.cloned.1.call-update) | async-done | bytes 4194320 | tf_op jit(solution)/shard_map/all_gather | solution.py:135
  224.2 8.2 %select_add_fusion = f32[1024,1024]{1,0:T(8,128)S(1)} fusion(f32[1024]{0:T(1024)S(1)} %fusion.44, bf16[2048,1024]{0,1:T(8,128)(2,1)} %all-gather.2.cloned.1.call-done), kind=kOutput, calls=%fused_computation.5 | convolution fusion | flops 4298113024 | bytes 8392704 | tf_op jit(solution)/shard_map/dot_general | solution.py:136
  232.4 2.0 copy-done.8
  235.0 18.2 %shard_map.64 = f32[128,128]{1,0:T(8,128)} custom-call(f32[128,128]{1,0:T(8,128)} %slice.183.d_ref), custom_call_target="tpu_custom_call" | custom-call | flops 12582912 | bytes 131072 | tf_op jit(solution)/shard_map/pallas_call | solution.py:64
  253.3 1.5 fusion.15
  255.6 4.6 %slice_subtract_fusion = f32[896,896]{1,0:T(8,128)S(1)} fusion(f32[1024,1024]{1,0:T(8,128)} %copy-done.8, f32[896,128]{1,0:T(8,128)S(1)} %fusion.15), kind=kOutput, calls=%fused_computation.7 | convolution fusion | flops 1233928192 | bytes 7340032 | tf_op jit(solution)/shard_map/dot_general | solution.py:88
  260.8 18.2 %shard_map.65 = f32[128,128]{1,0:T(8,128)} custom-call(f32[128,128]{1,0:T(8,128)} %slice.187.d_ref), custom_call_target="tpu_custom_call" | custom-call | flops 12582912 | bytes 131072 | tf_op jit(solution)/shard_map/pallas_call | solution.py:64
  279.1 1.3 fusion.17
  280.4 2.0 slice_subtract_fusion.1
  282.5 1.4 copy-done.2
  284.5 18.3 %shard_map.66 = f32[128,128]{1,0:T(8,128)} custom-call(f32[128,128]{1,0:T(8,128)} %slice.192.d_ref), custom_call_target="tpu_custom_call" | custom-call | flops 12582912 | bytes 131072 | tf_op jit(solution)/shard_map/pallas_call | solution.py:64
  302.8 1.4 fusion.19
  304.2 2.9 slice_subtract_fusion.2
  307.7 18.2 %shard_map.67 = f32[128,128]{1,0:T(8,128)} custom-call(f32[128,128]{1,0:T(8,128)} %slice.197.d_ref), custom_call_target="tpu_custom_call" | custom-call | flops 12582912 | bytes 131072 | tf_op jit(solution)/shard_map/pallas_call | solution.py:64
  329.8 18.2 %shard_map.68 = f32[128,128]{1,0:T(8,128)} custom-call(f32[128,128]{1,0:T(8,128)} %slice.202.d_ref), custom_call_target="tpu_custom_call" | custom-call | flops 12582912 | bytes 131072 | tf_op jit(solution)/shard_map/pallas_call | solution.py:64
  349.4 1.7 convolution_subtract_fusion.1
  351.7 18.2 %shard_map.69 = f32[128,128]{1,0:T(8,128)} custom-call(f32[128,128]{1,0:T(8,128)} %slice.207.d_ref), custom_call_target="tpu_custom_call" | custom-call | flops 12582912 | bytes 131072 | tf_op jit(solution)/shard_map/pallas_call | solution.py:64
  372.2 18.2 %shard_map.70 = f32[128,128]{1,0:T(8,128)} custom-call(f32[128,128]{1,0:T(8,128)} %slice.212.d_ref), custom_call_target="tpu_custom_call" | custom-call | flops 12582912 | bytes 131072 | tf_op jit(solution)/shard_map/pallas_call | solution.py:64
  396.6 18.2 %shard_map.71 = f32[128,128]{1,0:T(8,128)} custom-call(f32[128,128]{1,0:T(8,128)} %convolution_subtract_fusion.10.d_ref), custom_call_target="tpu_custom_call" | custom-call | flops 12582912 | bytes 131072 | tf_op jit(solution)/shard_map/pallas_call | solution.py:64
  (90 shorter events, 31.9 us)
Async XLA Ops:
  6.5 158.5 %reduce-scatter.2.cloned.1.call-start = ((), (), s32[]{:S(2)}) async-start(), calls=%async_computation.1 | async-start | bytes 8912896 | tf_op jit(solution)/shard_map/reduce_scatter | solution.py:129
  16.7 2.0 copy-start
  18.7 8.3 %copy-start.16 = (f32[2,8,128]{2,1,0:T(8,128)S(1)}, f32[2,8,128]{2,1,0:T(8,128)}, u32[]{:S(2)}) copy-start(f32[2,8,128]{2,1,0:T(8,128)} %param.10) | copy-start | bytes 24580
  18.9 8.2 %collective-permute-start.1 = (bf16[128,4,512]{2,0,1:T(8,128)(2,1)S(1)}, bf16[128,4,512]{2,0,1:T(8,128)(2,1)S(1)}, u32[]{:S(2)}, u32[]{:S(2)}) collective-permute-start(bf16[128,4,512]{2,0,1:T(8,128)(2,1)S(1)} %get-tuple-element.11), channel_id=1, source_target_pairs={{16,0},{32,16},{48,32},{64,48},{80,64},{96,80},{112,96},{17,1},{33... | collective-permute-start | bytes 1572872 | tf_op jit(solution)/shard_map/ppermute | solution.py:17
  20.2 6.9 %collective-permute-start.3 = (bf16[128,4,512]{2,0,1:T(8,128)(2,1)S(1)}, bf16[128,4,512]{2,0,1:T(8,128)(2,1)S(1)}, u32[]{:S(2)}, u32[]{:S(2)}) collective-permute-start(bf16[128,4,512]{2,0,1:T(8,128)(2,1)S(1)} %get-tuple-element.12), channel_id=1, source_target_pairs={{0,16},{16,32},{32,48},{48,64},{64,80},{80,96},{96,112},{1,17},{17... | collective-permute-start | bytes 1572872 | tf_op jit(solution)/shard_map/ppermute | solution.py:17
  25.2 11.2 %copy-start.1 = (bf16[1024,4,512]{2,0,1:T(8,128)(2,1)S(1)}, bf16[1024,4,512]{2,0,1:T(8,128)(2,1)}, u32[]{:S(2)}) copy-start(bf16[1024,4,512]{2,0,1:T(8,128)(2,1)} %copy-done) | copy-start | bytes 12582916
  29.1 11.3 %collective-permute-start = (bf16[128,4,512]{2,0,1:T(8,128)(2,1)S(1)}, bf16[128,4,512]{2,0,1:T(8,128)(2,1)S(1)}, u32[]{:S(2)}, u32[]{:S(2)}) collective-permute-start(bf16[128,4,512]{2,0,1:T(8,128)(2,1)S(1)} %get-tuple-element.10), channel_id=1, source_target_pairs={{16,0},{32,16},{48,32},{64,48},{80,64},{96,80},{112,96},{17,1},{33... | collective-permute-start | bytes 1572872 | tf_op jit(solution)/shard_map/ppermute | solution.py:17
  30.4 21.4 %collective-permute-start.2 = (bf16[128,4,512]{2,0,1:T(8,128)(2,1)S(1)}, bf16[128,4,512]{2,0,1:T(8,128)(2,1)S(1)}, u32[]{:S(2)}, u32[]{:S(2)}) collective-permute-start(bf16[128,4,512]{2,0,1:T(8,128)(2,1)S(1)} %get-tuple-element.8), channel_id=1, source_target_pairs={{0,16},{16,32},{32,48},{48,64},{64,80},{80,96},{96,112},{1,17},{17... | collective-permute-start | bytes 1572872 | tf_op jit(solution)/shard_map/ppermute | solution.py:17
  74.1 92.8 %copy-start.17 = (s32[8]{0:T(128)S(1)}, s32[8]{0:T(128)}, u32[]{:S(2)}) copy-start(s32[8]{0:T(128)} %param.11) | copy-start | bytes 100
  74.1 150.1 %all-gather.2.cloned.1.call-start = ((), (), s32[]{:S(2)}) async-start(), calls=%async_computation.2 | async-start | bytes 4456448 | tf_op jit(solution)/shard_map/all_gather | solution.py:135
  232.4 2.0 copy-start.8
  254.8 0.8 copy-start.3
  280.4 2.0 copy-start.5
  282.4 1.4 copy-start.2
  307.1 84.6 %copy-start.15 = (f32[128,128]{1,0:T(8,128)S(1)}, f32[128,128]{1,0:T(8,128)}, u32[]{:S(2)}) copy-start(f32[128,128]{1,0:T(8,128)} %shard_map.64) | copy-start | bytes 196612
  307.1 84.7 %copy-start.4 = (f32[896,128]{1,0:T(8,128)S(1)}, f32[896,128]{1,0:T(8,128)}, u32[]{:S(2)}) copy-start(f32[896,128]{1,0:T(8,128)} %copy-done.3) | copy-start | bytes 1376260
  327.2 65.2 %copy-start.14 = (f32[128,128]{1,0:T(8,128)S(1)}, f32[128,128]{1,0:T(8,128)}, u32[]{:S(2)}) copy-start(f32[128,128]{1,0:T(8,128)} %shard_map.65) | copy-start | bytes 196612
  327.2 65.4 %copy-start.6 = (f32[768,128]{1,0:T(8,128)S(1)}, f32[768,128]{1,0:T(8,128)}, u32[]{:S(2)}) copy-start(f32[768,128]{1,0:T(8,128)} %copy-done.5) | copy-start | bytes 1179652
  328.2 1.0 copy-start.7
  329.2 63.8 %copy-start.13 = (f32[128,128]{1,0:T(8,128)S(1)}, f32[128,128]{1,0:T(8,128)}, u32[]{:S(2)}) copy-start(f32[128,128]{1,0:T(8,128)} %shard_map.66) | copy-start | bytes 196612
  329.2 64.5 %copy-start.12 = (f32[128,128]{1,0:T(8,128)S(1)}, f32[128,128]{1,0:T(8,128)}, u32[]{:S(2)}) copy-start(f32[128,128]{1,0:T(8,128)} %shard_map.67) | copy-start | bytes 196612
  349.3 44.9 %copy-start.11 = (f32[128,128]{1,0:T(8,128)S(1)}, f32[128,128]{1,0:T(8,128)}, u32[]{:S(2)}) copy-start(f32[128,128]{1,0:T(8,128)} %shard_map.68) | copy-start | bytes 196612
  370.0 24.8 %copy-start.10 = (f32[128,128]{1,0:T(8,128)S(1)}, f32[128,128]{1,0:T(8,128)}, u32[]{:S(2)}) copy-start(f32[128,128]{1,0:T(8,128)} %shard_map.69) | copy-start | bytes 196612
  390.4 5.8 %copy-start.9 = (f32[128,128]{1,0:T(8,128)S(1)}, f32[128,128]{1,0:T(8,128)}, u32[]{:S(2)}) copy-start(f32[128,128]{1,0:T(8,128)} %shard_map.70) | copy-start | bytes 196612
Sparse Core Ops, SparseCore 0:
  74.2 90.8 reduce-scatter.1
  167.2 56.9 all-gather.1

commit v3 on v1

v3 whole, which is shorter than its diff:
```python
import math

import jax
import jax.numpy as jnp
from jax import lax
from jax.experimental import pallas as pl
from jax.sharding import PartitionSpec as P

KOUT = 2048
BLOCK = 128
PHASE = 8
HI = lax.Precision.HIGHEST


def shifted(x, axis, by):
    size = lax.axis_size(axis)
    pairs = [(i, i + by) for i in range(size) if 0 <= i + by < size]
    return lax.ppermute(x, axis, pairs)


def frame_start(live, rows, span):
    return jnp.minimum((live - 2 * span) // 16 * 16, rows - 2 * span - 16)

def shift_rows(buf, by, length):
    lead = length
    ext = jnp.concatenate([jnp.zeros((lead,) + buf.shape[1:], buf.dtype), buf,
                           jnp.zeros((length,) + buf.shape[1:], buf.dtype)], 0)
    return lax.dynamic_slice_in_dim(ext, lead + by, length, 0)

def take_angles(vec, idx, valid):
    return jnp.where(valid, jnp.take(vec, jnp.clip(idx, 0, vec.shape[0] - 1)), 0.0)

def build_block(amplitudes, sector_rows, moves, angles):
    sector_id = lax.axis_index("sector")
    nsec = lax.axis_size("sector")
    rows = amplitudes.shape[0]
    span = angles.shape[-1]
    live = sector_rows[sector_id]
    prev_id = jnp.maximum(sector_id - 1, 0)
    live_prev = sector_rows[prev_id]
    m0h, m1h = moves[0, sector_id], moves[1, sector_id]
    m0p = jnp.where(sector_id > 0, moves[0, prev_id], 0)
    m1p = jnp.where(sector_id > 0, moves[1, prev_id], 0)
    row_index = jnp.arange(rows)
    masked = jnp.where((row_index < live)[:, None, None], amplitudes, jnp.zeros((), amplitudes.dtype))
    a_len = 2 * span + 16
    b_len = 2 * span
    fa = frame_start(live, rows, span)
    fa_prev = frame_start(live_prev, rows, span)
    a_frame = lax.dynamic_slice_in_dim(masked, fa, a_len, 0)
    b_frame = masked[:b_len]
    from_below = shifted(a_frame, "sector", 1)
    from_above = shifted(b_frame, "sector", -1)
    j = jnp.arange(a_len)
    i0 = j + fa - live + m0h
    i1 = j + fa - live + m0h + m1h
    v0 = (i0 >= 0) & (i0 < m0h)
    v1 = (i1 >= 0) & (i1 < m1h)
    p0 = shift_rows(from_above, fa - live + m0h, a_len)
    p1 = shift_rows(from_above, fa - live + 2 * m0h + m1h, a_len)
    ang = take_angles(angles[0][sector_id], i0, v0) + take_angles(angles[1][sector_id], i1, v1)
    partner = jnp.where(v0[:, None, None], p0, p1).astype(jnp.float32)
    own = a_frame.astype(jnp.float32)
    c = jnp.cos(ang)[:, None, None]
    s = jnp.sin(ang)[:, None, None]
    new_a = jnp.where((v0 | v1)[:, None, None], c * own - s * partner, own).astype(jnp.bfloat16)
    jb = jnp.arange(b_len)
    k0 = jb
    k1 = jb - m0p
    w0 = k0 < m0p
    w1 = (k1 >= 0) & (k1 < m1p)
    q0 = shift_rows(from_below, live_prev - m0p - fa_prev, b_len)
    q1 = shift_rows(from_below, live_prev - 2 * m0p - m1p - fa_prev, b_len)
    angb = take_angles(angles[0][prev_id], k0, w0) + take_angles(angles[1][prev_id], k1, w1)
    partner_b = jnp.where(w0[:, None, None], q0, q1).astype(jnp.float32)
    ownb = b_frame.astype(jnp.float32)
    cb = jnp.cos(angb)[:, None, None]
    sb = jnp.sin(angb)[:, None, None]
    new_b = jnp.where((w0 | w1)[:, None, None], sb * partner_b + cb * ownb, ownb).astype(jnp.bfloat16)
    block = lax.dynamic_update_slice_in_dim(masked, new_a, fa, 0)
    return lax.dynamic_update_slice_in_dim(block, new_b, 0, 0)


def dot(a, b):
    return jnp.dot(a, b, precision=HI, preferred_element_type=jnp.float32)


def factor_inverse_kernel(d_ref, o_ref):
    n = d_ref.shape[0]
    a = d_ref[...]
    eye_rows = lax.broadcasted_iota(jnp.int32, (n, n), 0)
    w = (eye_rows == lax.broadcasted_iota(jnp.int32, (n, n), 1)).astype(jnp.float32)
    for first in range(0, n, PHASE):
        m = n - first
        lane = lax.broadcasted_iota(jnp.int32, (m, n), 1)
        sub = lax.broadcasted_iota(jnp.int32, (m, n), 0)
        lane_row = lax.broadcasted_iota(jnp.int32, (1, n), 1)
        sub_col = lax.broadcasted_iota(jnp.int32, (m, 1), 0)

        def body(t, carry, first=first, lane=lane, sub=sub, lane_row=lane_row, sub_col=sub_col):
            a, w = carry
            j = first + t
            col = jnp.sum(jnp.where(lane == j, a, 0.0), axis=1, keepdims=True)
            row = jnp.sum(jnp.where(sub == t, a, 0.0), axis=0, keepdims=True)
            piv = jnp.sum(jnp.where(lane_row == j, row, 0.0), axis=1, keepdims=True)
            r = lax.rsqrt(piv)
            lcol = jnp.where(sub_col >= t, col * r, 0.0)
            lrow = jnp.where(lane_row >= j, row * r, 0.0)
            a = a - lcol * lrow
            wj = jnp.sum(jnp.where(sub == t, w, 0.0), axis=0, keepdims=True) * r
            w = jnp.where(sub == t, wj, w - lcol * wj)
            return a, w

        a, w = lax.fori_loop(0, PHASE, body, (a, w), unroll=PHASE)
        o_ref[first:first + PHASE, :] = w[:PHASE]
        a = a[PHASE:]
        w = w[PHASE:]


def factor_inverse(diag):
    n = diag.shape[0]
    return pl.pallas_call(
        factor_inverse_kernel,
        out_shape=jax.ShapeDtypeStruct((n, n), jnp.float32),
        cost_estimate=pl.CostEstimate(
            flops=6 * n * n * n, transcendentals=n, bytes_accessed=8 * n * n
        ),
    )(diag)


def cholesky_solve(gram, rhs):
    n = gram.shape[0]
    trailing = gram
    rest = rhs
    solved = []
    for start in range(0, n, BLOCK):
        diag = trailing[:BLOCK, :BLOCK]
        inverse = factor_inverse(diag)
        head = dot(inverse, rest[:BLOCK])
        solved.append(head)
        if start + BLOCK < n:
            panel = lax.dot_general(
                trailing[BLOCK:, :BLOCK], inverse, (((1,), (1,)), ((), ())),
                precision=HI, preferred_element_type=jnp.float32,
            )
            trailing = trailing[BLOCK:, BLOCK:] - lax.dot_general(
                panel, panel, (((1,), (1,)), ((), ())),
                precision=HI, preferred_element_type=jnp.float32,
            )
            rest = rest[BLOCK:] - dot(panel, head)
    return jnp.concatenate(solved, 0)


def per_device(amplitudes, next_site, sector_rows, moves, angles, ranks):
    sector_id = lax.axis_index("sector")
    rows = amplitudes.shape[0]
    row_index = jnp.arange(rows)
    live_rows = sector_rows[sector_id]
    block_rows = build_block(amplitudes, sector_rows, moves, angles)
    site_tensor = next_site[0]
    contracted = lax.psum_scatter(
        jnp.einsum("prk,lpr->kl", site_tensor, block_rows, preferred_element_type=jnp.float32),
        "row",
        scatter_dimension=0,
        tiled=True,
    ).astype(jnp.bfloat16)
    gathered = lax.all_gather(contracted, "row", axis=0, tiled=True)
    gram_matrix = lax.dot_general(
        gathered, gathered, (((0,), (0,)), ((), ())), preferred_element_type=jnp.float32
    )
    dead_rows = (row_index >= live_rows).astype(jnp.float32)
    gram_matrix = gram_matrix + jnp.diag(dead_rows)
    solved = cholesky_solve(gram_matrix, contracted.astype(jnp.float32).T).T
    kept_mask = ((row_index >= live_rows - ranks[sector_id]) & (row_index < live_rows)).astype(
        jnp.float32
    )
    return (solved * math.sqrt(KOUT) * kept_mask[None, :]).astype(jnp.bfloat16)


def solution(mesh):
    placed = (P("sector", None, "row"), P("sector", None, "row", None), P(), P(), P(), P())
    return jax.shard_map(
        per_device, mesh=mesh, in_specs=placed, out_specs=P("row", "sector"), check_vma=False
    )
```

time: 478 us -> 418 us (0.87)
  other arithmetic: 208 us -> 40.4 us
  Pallas kernels: 0 us -> 116 us
  starting transfers between devices: 11.8 us -> 4.66 us
    another operation x40 -> x0, other arithmetic: 186 us -> none  [the longest x24 101 us: cholesky_solve(): factor = jnp.linalg.cholesky(diag)]
    pallas_call x0 -> x8, Pallas kernels: none -> 116 us  [factor_inverse(): pl.pallas_call(factor_inverse_kernel, out_shape=jax.ShapeDtypeStruct((n,...]
    concatenate x0 -> x2, other arithmetic: none -> 16.8 us  [shift_rows(): jnp.concatenate([jnp.zeros((lead,) + buf.shape[1:], buf.dtype), buf, jnp....]
    dynamic_update_slice x3 -> x0, local copies, waits for them, and re-layouts: 16.7 us -> none  [the longest x1 5.57 us: per_device(): padded = lax.dynamic_update_slice_in_dim(padded, new_a[1], starts_a[1], 0)]
    gather x0 -> x4, local copies, waits for them, and re-layouts: none -> 8.45 us  [take_angles(): jnp.take(vec, jnp.clip(idx, 0, vec.shape[0] - 1))]
    ppermute x4 -> x2, starting transfers between devices: 11.8 us -> 4.62 us  [shifted(): return lax.ppermute(x, axis, pairs)]
    unnamed x32 -> x39, local copies, waits for them, and re-layouts: 8.85 us -> 12.1 us
  transfers between devices with their start and end apart: 6 -> 4, of which waited for: 2 -> 2; matrix products, arithmetic and copies ran while one was open for 4% -> 6% of each run, Pallas kernels for 0% -> 0%
where the time goes in v3:
time: 418 us; the launch traced here: 410 us
  waiting for transfers between devices  148 us (35%)
  Pallas kernels  116 us (28%)
  matrix products  50 us (12%)
  other arithmetic  40.4 us (10%)
  local copies, waits for them, and re-layouts  29.5 us (7%)
  between operations  21.9 us (5%)
  starting transfers between devices  4.66 us (1%)
    pallas_call x8, Pallas kernels, factor_inverse(): pl.pallas_call(factor_inverse_kernel, out_shape=jax.ShapeDtypeStruct((n,...  116 us
    reduce_scatter x1, waiting for transfers between devices, per_device(): lax.psum_scatter(jnp.einsum('prk,lpr->kl', site_tensor, block_rows, prefe...  94.6 us
    all_gather x1, waiting for transfers between devices, per_device(): gathered = lax.all_gather(contracted, 'row', axis=0, tiled=True)  53.2 us
    concatenate x2, other arithmetic, shift_rows(): jnp.concatenate([jnp.zeros((lead,) + buf.shape[1:], buf.dtype), buf, jnp....  16.8 us
    dot_general x7, matrix products, cholesky_solve(): lax.dot_general(panel, panel, (((1,), (1,)), ((), ())), precision=HI, pre...  13.8 us
    dot_general x1, matrix products, per_device(): jnp.einsum('prk,lpr->kl', site_tensor, block_rows, preferred_element_type...  13.3 us
    unnamed x39, local copies, waits for them, and re-layouts  12.1 us
    dot_general x7, matrix products, cholesky_solve(): lax.dot_general(trailing[BLOCK:, :BLOCK], inverse, (((1,), (1,)), ((), ()...  8.98 us
  transfers between devices with their start and end apart: 4, of which 2 were waited for; matrix products, arithmetic and copies ran while one was open for 6% of the time, Pallas kernels for 0%

profile of v3, /device:TPU:0, one launch (start us, length us, event | category | flops | bytes accessed | tf_op | source)
XLA Modules:
  0.0 410.2 jit_solution(1811544372177826350)
XLA Ops:
  8.4 5.3 %broadcast_select_fusion = bf16[1024,4,512]{2,1,0:T(4,128)(2,1)S(1)} fusion(bf16[1024,4,512]{2,1,0:T(4,128)(2,1)} %param.10, pred[1024]{0:T(1024)(128)(4,1)S(1)} %iota_compare_fusion.3), kind=kLoop, calls=%fused_computation.10 | loop fusion | flops 2097152 | bytes 8389632 | tf_op jit(solution)/shard_map/jit(_where)/select_n | solution.py:45
  13.8 2.0 copy-done
  21.0 5.7 %copy.13 = bf16[1024,4,512]{2,1,0:T(4,128)(2,1)} copy(bf16[1024,4,512]{2,1,0:T(4,128)(2,1)} %copy-done) | data formatting | bytes 8388608
  28.4 2.4 gather_fusion
  30.8 2.4 gather_fusion.1
  33.1 1.7 fusion.62
  34.8 1.8 fusion.65
  37.0 8.5 %pad_maximum_fusion = bf16[800,4,512]{2,1,0:T(4,128)(2,1)S(1)} fusion(bf16[272,4,512]{2,1,0:T(4,128)(2,1)S(1)} %broadcast.108, bf16[256,4,512]{2,1,0:T(4,128)(2,1)S(1)} %collective-permute-done), kind=kLoop, calls=%fused_computation.11 | loop fusion | flops 3276800 | bytes 5439488 | tf_op jit(solution)/shard_map/concatenate | solution.py:26
  45.5 4.4 %constant_dynamic-slice_fusion.3 = (bf16[272,4,512]{2,1,0:T(4,128)(2,1)S(1)}, bf16[1024,4,512]{2,1,0:T(4,128)(2,1)}) fusion(bf16[1024,4,512]{2,1,0:T(4,128)(2,1)} %copy.13, s32[]{:T(128)S(6)} %select_n.103, bf16[800,4,512]{2,1,0:T(4,128)(2,1)S(1)} %pad_maximum_fusion, s32[]{:T(128)S(6)} %select_n.105, s32[]{:T(128)S(6)} %select_n.104, ...), kind=kLoop, calls=%fused_computation.92 | loop fusion | flops 4456448 | bytes 5573292 | tf_op jit(solution)/shard_map/dynamic_slice | solution.py:50
  49.9 3.3 collective-permute-start.1
  56.5 1.9 gather_fusion.2
  58.4 1.9 gather_fusion.3
  60.7 8.3 %pad_maximum_fusion.1 = bf16[784,4,512]{2,1,0:T(4,128)(2,1)S(1)} fusion(bf16[256,4,512]{2,1,0:T(4,128)(2,1)S(1)} %broadcast.109, bf16[272,4,512]{2,1,0:T(4,128)(2,1)S(1)} %collective-permute-done.1), kind=kLoop, calls=%fused_computation.13 | loop fusion | flops 3211264 | bytes 5373952 | tf_op jit(solution)/shard_map/concatenate | solution.py:26
  69.1 3.8 fusion.11
  72.9 13.3 %fusion.2 = f32[2048,1024]{0,1:T(8,128)} fusion(bf16[1,4,512,2048]{3,2,1,0:T(8,128)(2,1)} %param.11, bf16[1024,4,512]{2,1,0:T(4,128)(2,1)S(1)} %fusion.11), kind=kOutput, calls=%fused_computation.6 | convolution fusion | flops 8589934592 | bytes 20971520 | tf_op jit(solution)/shard_map/prk,lpr->kl/dot_general | solution.py:162
  86.3 94.6 %reduce-scatter.2.cloned.1.call-done = f32[128,1024]{0,1:T(8,128)} async-done(((f32[2048,1024]{0,1:T(8,128)}), f32[128,1024]{0,1:T(8,128)}) %reduce-scatter.2.cloned.1.call-update) | async-done | bytes 524304 | tf_op jit(solution)/shard_map/reduce_scatter | solution.py:161
  180.8 1.8 convert_element_type.46
  186.7 53.2 %all-gather.2.cloned.1.call-done = bf16[2048,1024]{0,1:T(8,128)(2,1)} async-done(((bf16[128,1024]{0,1:T(8,128)(2,1)}), bf16[2048,1024]{0,1:T(8,128)(2,1)}) %all-gather.2.cloned.1.call-update) | async-done | bytes 4194320 | tf_op jit(solution)/shard_map/all_gather | solution.py:167
  240.0 8.6 %select_add_fusion = f32[1024,1024]{1,0:T(8,128)S(1)} fusion(f32[1024]{0:T(1024)S(1)} %fusion.41, bf16[2048,1024]{0,1:T(8,128)(2,1)} %all-gather.2.cloned.1.call-done), kind=kOutput, calls=%fused_computation.8 | convolution fusion | flops 4298113024 | bytes 8392704 | tf_op jit(solution)/shard_map/dot_general | solution.py:168
  248.6 2.0 copy-done.8
  251.2 14.5 %shard_map.64 = f32[128,128]{1,0:T(8,128)} custom-call(f32[128,128]{1,0:T(8,128)} %slice.167.d_ref), custom_call_target="tpu_custom_call" | custom-call | flops 12582912 | bytes 131072 | tf_op jit(solution)/shard_map/pallas_call | solution.py:122
  267.3 4.7 %slice_subtract_fusion = f32[896,896]{1,0:T(8,128)S(1)} fusion(f32[1024,1024]{1,0:T(8,128)} %copy-done.8, f32[896,128]{1,0:T(8,128)S(1)} %fusion.12), kind=kOutput, calls=%fused_computation.12 | convolution fusion | flops 1233928192 | bytes 7340032 | tf_op jit(solution)/shard_map/dot_general | solution.py:146
  272.7 14.5 %shard_map.65 = f32[128,128]{1,0:T(8,128)} custom-call(f32[128,128]{1,0:T(8,128)} %slice.171.d_ref), custom_call_target="tpu_custom_call" | custom-call | flops 12582912 | bytes 131072 | tf_op jit(solution)/shard_map/pallas_call | solution.py:122
  288.5 2.2 slice_subtract_fusion.1
  292.8 14.5 %shard_map.66 = f32[128,128]{1,0:T(8,128)} custom-call(f32[128,128]{1,0:T(8,128)} %slice.176.d_ref), custom_call_target="tpu_custom_call" | custom-call | flops 12582912 | bytes 131072 | tf_op jit(solution)/shard_map/pallas_call | solution.py:122
  308.6 2.9 slice_subtract_fusion.2
  312.2 14.5 %shard_map.67 = f32[128,128]{1,0:T(8,128)} custom-call(f32[128,128]{1,0:T(8,128)} %slice.181.d_ref), custom_call_target="tpu_custom_call" | custom-call | flops 12582912 | bytes 131072 | tf_op jit(solution)/shard_map/pallas_call | solution.py:122
  330.5 14.7 %shard_map.68 = f32[128,128]{1,0:T(8,128)} custom-call(f32[128,128]{1,0:T(8,128)} %slice.186.d_ref), custom_call_target="tpu_custom_call" | custom-call | flops 12582912 | bytes 131072 | tf_op jit(solution)/shard_map/pallas_call | solution.py:122
  346.5 1.7 convolution_subtract_fusion.1
  348.9 14.5 %shard_map.69 = f32[128,128]{1,0:T(8,128)} custom-call(f32[128,128]{1,0:T(8,128)} %slice.191.d_ref), custom_call_target="tpu_custom_call" | custom-call | flops 12582912 | bytes 131072 | tf_op jit(solution)/shard_map/pallas_call | solution.py:122
  365.5 14.5 %shard_map.70 = f32[128,128]{1,0:T(8,128)} custom-call(f32[128,128]{1,0:T(8,128)} %slice.196.d_ref), custom_call_target="tpu_custom_call" | custom-call | flops 12582912 | bytes 131072 | tf_op jit(solution)/shard_map/pallas_call | solution.py:122
  386.4 14.5 %shard_map.71 = f32[128,128]{1,0:T(8,128)} custom-call(f32[128,128]{1,0:T(8,128)} %convolution_subtract_fusion.10.d_ref), custom_call_target="tpu_custom_call" | custom-call | flops 12582912 | bytes 131072 | tf_op jit(solution)/shard_map/pallas_call | solution.py:122
  (99 shorter events, 34.0 us)
Async XLA Ops:
  6.5 174.3 %reduce-scatter.2.cloned.1.call-start = ((), (), s32[]{:S(2)}) async-start(), calls=%async_computation.1 | async-start | bytes 8912896 | tf_op jit(solution)/shard_map/reduce_scatter | solution.py:161
  8.4 10.1 %copy-start.17 = (s32[2,8]{1,0:T(2,128)S(1)}, s32[2,8]{1,0:T(2,128)}, u32[]{:S(2)}) copy-start(s32[2,8]{1,0:T(2,128)} %param.13) | copy-start | bytes 196
  13.8 2.0 copy-start
  16.1 20.6 %collective-permute-start = (bf16[256,4,512]{2,1,0:T(4,128)(2,1)S(1)}, bf16[256,4,512]{2,1,0:T(4,128)(2,1)S(1)}, u32[]{:S(2)}, u32[]{:S(2)}) collective-permute-start(bf16[256,4,512]{2,1,0:T(4,128)(2,1)S(1)} %slice.166), channel_id=1, source_target_pairs={{16,0},{32,16},{48,32},{64,48},{80,64},{96,80},{112,96},{17,1},{33... | collective-permute-start | bytes 3145736 | tf_op jit(solution)/shard_map/ppermute | solution.py:18
  20.9 5.7 %copy-start.16 = (f32[2,8,128]{2,1,0:T(8,128)S(1)}, f32[2,8,128]{2,1,0:T(8,128)}, u32[]{:S(2)}) copy-start(f32[2,8,128]{2,1,0:T(8,128)} %param.14) | copy-start | bytes 24580
  49.9 10.5 %collective-permute-start.1 = (bf16[272,4,512]{2,1,0:T(4,128)(2,1)S(1)}, bf16[272,4,512]{2,1,0:T(4,128)(2,1)S(1)}, u32[]{:S(2)}, u32[]{:S(2)}) collective-permute-start(bf16[272,4,512]{2,1,0:T(4,128)(2,1)S(1)} %get-tuple-element.14), channel_id=1, source_target_pairs={{0,16},{16,32},{32,48},{48,64},{64,80},{80,96},{96,112},{1,17},{17... | collective-permute-start | bytes 3342344 | tf_op jit(solution)/shard_map/ppermute | solution.py:18
  60.4 8.6 %copy-start.4 = (bf16[1024,4,512]{2,1,0:T(4,128)(2,1)S(1)}, bf16[1024,4,512]{2,1,0:T(4,128)(2,1)}, u32[]{:S(2)}) copy-start(bf16[1024,4,512]{2,1,0:T(4,128)(2,1)} %get-tuple-element.15) | copy-start | bytes 12582916
  86.2 96.4 %copy-start.18 = (s32[8]{0:T(128)S(1)}, s32[8]{0:T(128)}, u32[]{:S(2)}) copy-start(s32[8]{0:T(128)} %param.15) | copy-start | bytes 100
  86.2 153.8 %all-gather.2.cloned.1.call-start = ((), (), s32[]{:S(2)}) async-start(), calls=%async_computation.2 | async-start | bytes 4456448 | tf_op jit(solution)/shard_map/all_gather | solution.py:167
  248.6 2.0 copy-start.8
  267.2 4.8 %copy-start.2 = (f32[896,128]{1,0:T(8,128)}, f32[896,128]{1,0:T(8,128)S(1)}, u32[]{:S(2)}) copy-start(f32[896,128]{1,0:T(8,128)S(1)} %fusion.12) | copy-start | bytes 1376260
  288.5 2.2 copy-start.5
  290.7 1.4 copy-start.1
  327.8 53.2 %copy-start.15 = (f32[128,128]{1,0:T(8,128)S(1)}, f32[128,128]{1,0:T(8,128)}, u32[]{:S(2)}) copy-start(f32[128,128]{1,0:T(8,128)} %shard_map.64) | copy-start | bytes 196612
  327.9 53.4 %copy-start.3 = (f32[896,128]{1,0:T(8,128)S(1)}, f32[896,128]{1,0:T(8,128)}, u32[]{:S(2)}) copy-start(f32[896,128]{1,0:T(8,128)} %copy-done.2) | copy-start | bytes 1376260
  328.9 1.0 copy-start.7
  329.9 52.2 %copy-start.14 = (f32[128,128]{1,0:T(8,128)S(1)}, f32[128,128]{1,0:T(8,128)}, u32[]{:S(2)}) copy-start(f32[128,128]{1,0:T(8,128)} %shard_map.65) | copy-start | bytes 196612
  329.9 52.4 %copy-start.6 = (f32[768,128]{1,0:T(8,128)S(1)}, f32[768,128]{1,0:T(8,128)}, u32[]{:S(2)}) copy-start(f32[768,128]{1,0:T(8,128)} %copy-done.5) | copy-start | bytes 1179652
  346.5 36.3 %copy-start.13 = (f32[128,128]{1,0:T(8,128)S(1)}, f32[128,128]{1,0:T(8,128)}, u32[]{:S(2)}) copy-start(f32[128,128]{1,0:T(8,128)} %shard_map.66) | copy-start | bytes 196612
  348.2 35.2 %copy-start.12 = (f32[128,128]{1,0:T(8,128)S(1)}, f32[128,128]{1,0:T(8,128)}, u32[]{:S(2)}) copy-start(f32[128,128]{1,0:T(8,128)} %shard_map.67) | copy-start | bytes 196612
  364.4 19.6 %copy-start.11 = (f32[128,128]{1,0:T(8,128)S(1)}, f32[128,128]{1,0:T(8,128)}, u32[]{:S(2)}) copy-start(f32[128,128]{1,0:T(8,128)} %shard_map.68) | copy-start | bytes 196612
  379.9 4.6 %copy-start.10 = (f32[128,128]{1,0:T(8,128)S(1)}, f32[128,128]{1,0:T(8,128)}, u32[]{:S(2)}) copy-start(f32[128,128]{1,0:T(8,128)} %shard_map.69) | copy-start | bytes 196612
  382.1 3.9 copy-start.9
Sparse Core Ops, SparseCore 0:
  86.3 94.4 reduce-scatter.1
  183.0 56.9 all-gather.1

commit v4 on v1

--- a/solution.py
+++ b/solution.py
@@ -3,10 +3,13 @@
 import jax
 import jax.numpy as jnp
 from jax import lax
+from jax.experimental import pallas as pl
 from jax.sharding import PartitionSpec as P
 
 KOUT = 2048
 BLOCK = 128
+PHASE = 16
+UNROLL = 4
 HI = lax.Precision.HIGHEST
 
 
@@ -33,16 +36,60 @@
     return jnp.dot(a, b, precision=HI, preferred_element_type=jnp.float32)
 
 
+def factor_inverse_kernel(d_ref, o_ref):
+    n = d_ref.shape[0]
+    a = d_ref[...]
+    rows_n = lax.broadcasted_iota(jnp.int32, (n, n), 0)
+    lanes_n = lax.broadcasted_iota(jnp.int32, (n, n), 1)
+    w = (rows_n == lanes_n).astype(jnp.float32)
+    diag = jnp.sum(jnp.where(rows_n == lanes_n, a, 0.0), axis=0, keepdims=True)
+    for first in range(0, n, PHASE):
+        m = n - first
+        lane = lax.broadcasted_iota(jnp.int32, (m, n), 1)
+        sub = lax.broadcasted_iota(jnp.int32, (m, n), 0)
+        lane_row = lax.broadcasted_iota(jnp.int32, (1, n), 1)
+        sub_col = lax.broadcasted_iota(jnp.int32, (m, 1), 0)
+
+        def body(t, carry, first=first, lane=lane, sub=sub, lane_row=lane_row, sub_col=sub_col):
+            a, w, diag = carry
+            j = first + t
+            col = jnp.sum(jnp.where(lane == j, a, 0.0), axis=1, keepdims=True)
+            row = jnp.sum(jnp.where(sub == t, a, 0.0), axis=0, keepdims=True)
+            piv = jnp.sum(jnp.where(lane_row == j, diag, 0.0), axis=1, keepdims=True)
+            r = lax.rsqrt(piv)
+            lcol = jnp.where(sub_col >= t, col * r, 0.0)
+            lrow = jnp.where(lane_row >= j, row * r, 0.0)
+            a = a - lcol * lrow
+            diag = diag - lrow * lrow
+            wj = jnp.sum(jnp.where(sub == t, w, 0.0), axis=0, keepdims=True) * r
+            w = jnp.where(sub == t, wj, w - lcol * wj)
+            return a, w, diag
+
+        a, w, diag = lax.fori_loop(0, PHASE, body, (a, w, diag), unroll=UNROLL)
+        o_ref[first:first + PHASE, :] = w[:PHASE]
+        a = a[PHASE:]
+        w = w[PHASE:]
+
+
+def factor_inverse(diag):
+    n = diag.shape[0]
+    return pl.pallas_call(
+        factor_inverse_kernel,
+        out_shape=jax.ShapeDtypeStruct((n, n), jnp.float32),
+        cost_estimate=pl.CostEstimate(
+            flops=6 * n * n * n, transcendentals=n, bytes_accessed=8 * n * n
+        ),
+    )(diag)
+
+
 def cholesky_solve(gram, rhs):
     n = gram.shape[0]
-    eye = jnp.eye(BLOCK, dtype=jnp.float32)
     trailing = gram
     rest = rhs
     solved = []
     for start in range(0, n, BLOCK):
         diag = trailing[:BLOCK, :BLOCK]
-        factor = jnp.linalg.cholesky(diag)
-        inverse = lax.linalg.triangular_solve(factor, eye, left_side=True, lower=True)
+        inverse = factor_inverse(diag)
         head = dot(inverse, rest[:BLOCK])
         solved.append(head)
         if start + BLOCK < n:

time: 478 us -> 384 us (0.80); the launches traced: 470 us -> 383 us
  other arithmetic: 208 us -> 18.1 us
  Pallas kernels: 0 us -> 104 us
    another operation x40 -> x0, other arithmetic: 186 us -> none  [the longest x24 101 us: cholesky_solve(): factor = jnp.linalg.cholesky(diag)]
    pallas_call x0 -> x8, Pallas kernels: none -> 104 us  [factor_inverse(): pl.pallas_call(factor_inverse_kernel, out_shape=jax.ShapeDtypeStruct((n,...]
  transfers between devices with their start and end apart: 6 -> 6, of which waited for: 2 -> 2; matrix products, arithmetic and copies ran while one was open for 4% -> 5% of each run, Pallas kernels for 0% -> 0%
where the time goes in v4:
time: 384 us; the launch traced here: 383 us
  waiting for transfers between devices  144 us (38%)
  Pallas kernels  104 us (27%)
  matrix products  50.3 us (13%)
  local copies, waits for them, and re-layouts  34.4 us (9%)
  between operations  19 us (5%)
  other arithmetic  18.1 us (5%)
  starting transfers between devices  12 us (3%)
    pallas_call x8, Pallas kernels, factor_inverse(): pl.pallas_call(factor_inverse_kernel, out_shape=jax.ShapeDtypeStruct((n,...  104 us
    reduce_scatter x1, waiting for transfers between devices, per_device(): lax.psum_scatter(jnp.einsum('prk,lpr->kl', site_tensor, block_rows, prefe...  91 us
    all_gather x1, waiting for transfers between devices, per_device(): gathered = lax.all_gather(contracted, 'row', axis=0, tiled=True)  53.3 us
    dot_general x1, matrix products, per_device(): jnp.einsum('prk,lpr->kl', site_tensor, block_rows, preferred_element_type...  14.6 us
    dot_general x7, matrix products, cholesky_solve(): lax.dot_general(panel, panel, (((1,), (1,)), ((), ())), precision=HI, pre...  13.5 us
    ppermute x4, starting transfers between devices, shifted(): return lax.ppermute(x, axis, pairs)  11.7 us
    dot_general x7, matrix products, cholesky_solve(): lax.dot_general(trailing[BLOCK:, :BLOCK], inverse, (((1,), (1,)), ((), ()...  9.1 us
    dot_general x1, matrix products, per_device(): lax.dot_general(gathered, gathered, (((0,), (0,)), ((), ())), preferred_e...  8.17 us
  transfers between devices with their start and end apart: 6, of which 2 were waited for; matrix products, arithmetic and copies ran while one was open for 5% of the time, Pallas kernels for 0%

profile of v4, /device:TPU:0, one launch (start us, length us, event | category | flops | bytes accessed | tf_op | source)
XLA Modules:
  0.0 382.5 jit_solution(11334858943396379950)
XLA Ops:
  11.6 5.1 %copy_select_fusion = bf16[1024,4,512]{2,0,1:T(8,128)(2,1)S(1)} fusion(bf16[1024,4,512]{2,1,0:T(4,128)(2,1)} %param.6, pred[1024]{0:T(1024)(128)(4,1)S(1)} %iota_compare_fusion.3), kind=kLoop, calls=%fused_computation.4 | loop fusion | flops 2097152 | bytes 8389632 | tf_op jit(solution)/shard_map/jit(_where)/select_n | solution.py:117
  16.7 2.0 copy-done
  20.2 3.1 collective-permute-start.3
  27.1 2.0 fusion.9
  30.4 6.1 %collective-permute-start.2 = (bf16[128,4,512]{2,0,1:T(8,128)(2,1)S(1)}, bf16[128,4,512]{2,0,1:T(8,128)(2,1)S(1)}, u32[]{:S(2)}, u32[]{:S(2)}) collective-permute-start(bf16[128,4,512]{2,0,1:T(8,128)(2,1)S(1)} %get-tuple-element.8), channel_id=1, source_target_pairs={{0,16},{16,32},{32,48},{48,64},{64,80},{80,96},{96,112},{1,17},{17... | collective-permute-start | bytes 1572872 | tf_op jit(solution)/shard_map/ppermute | solution.py:19
  36.5 2.6 concatenate.6
  40.7 5.6 %dynamic_update_slice.12 = bf16[1152,4,512]{2,0,1:T(8,128)(2,1)} dynamic-update-slice(bf16[1152,4,512]{2,0,1:T(8,128)(2,1)} %concatenate.6, bf16[128,4,512]{2,0,1:T(8,128)(2,1)S(1)} %fusion.7, s32[]{:T(128)S(6)} %select_n.55, s32[]{:T(128)} %constant.22.clone.1, s32[]{:T(128)} %constant.22.clone.1) | dynamic-update-slice | bytes 1048580 | tf_op jit(solution)/shard_map/dynamic_update_slice | solution.py:135
  46.3 5.5 %dynamic_update_slice.13 = bf16[1152,4,512]{2,0,1:T(8,128)(2,1)} dynamic-update-slice(bf16[1152,4,512]{2,0,1:T(8,128)(2,1)} %dynamic_update_slice.12, bf16[128,4,512]{2,0,1:T(8,128)(2,1)S(1)} %get-tuple-element.7, s32[]{:T(128)S(6)} %select_n.60, s32[]{:T(128)} %constant.22.clone.1, s32[]{:T(128)} %constant.22.clone.1) | dynamic-update-slice | bytes 1048580 | tf_op jit(solution)/shard_map/dynamic_update_slice | solution.py:136
  51.8 2.2 fusion.14
  54.0 5.6 %dynamic_update_slice.15 = bf16[1152,4,512]{2,0,1:T(8,128)(2,1)} dynamic-update-slice(bf16[1152,4,512]{2,0,1:T(8,128)(2,1)} %fusion.14, bf16[128,4,512]{2,0,1:T(8,128)(2,1)S(1)} %get-tuple-element.9, s32[]{:T(128)S(6)} %select_n.58, s32[]{:T(128)} %constant.22.clone.1, s32[]{:T(128)} %constant.22.clone.1) | dynamic-update-slice | bytes 1048580 | tf_op jit(solution)/shard_map/dynamic_update_slice | solution.py:138
  59.5 14.6 %fusion.2 = f32[2048,1024]{0,1:T(8,128)} fusion(bf16[1,4,512,2048]{3,2,1,0:T(8,128)(2,1)} %param.7, bf16[1152,4,512]{2,0,1:T(8,128)(2,1)} %dynamic_update_slice.15), kind=kOutput, calls=%fused_computation.2 | convolution fusion | flops 8589934592 | bytes 20971520 | tf_op jit(solution)/shard_map/prk,lpr->kl/dot_general | solution.py:142
  74.4 91.0 %reduce-scatter.2.cloned.1.call-done = f32[128,1024]{0,1:T(8,128)} async-done(((f32[2048,1024]{0,1:T(8,128)}), f32[128,1024]{0,1:T(8,128)}) %reduce-scatter.2.cloned.1.call-update) | async-done | bytes 524304 | tf_op jit(solution)/shard_map/reduce_scatter | solution.py:141
  165.3 1.8 convert_element_type.70
  171.2 53.3 %all-gather.2.cloned.1.call-done = bf16[2048,1024]{0,1:T(8,128)(2,1)} async-done(((bf16[128,1024]{0,1:T(8,128)(2,1)}), bf16[2048,1024]{0,1:T(8,128)(2,1)}) %all-gather.2.cloned.1.call-update) | async-done | bytes 4194320 | tf_op jit(solution)/shard_map/all_gather | solution.py:147
  224.5 8.2 %select_add_fusion = f32[1024,1024]{1,0:T(8,128)S(1)} fusion(f32[1024]{0:T(1024)S(1)} %fusion.44, bf16[2048,1024]{0,1:T(8,128)(2,1)} %all-gather.2.cloned.1.call-done), kind=kOutput, calls=%fused_computation.5 | convolution fusion | flops 4298113024 | bytes 8392704 | tf_op jit(solution)/shard_map/dot_general | solution.py:148
  232.7 2.0 copy-done.8
  235.3 13.0 %shard_map.64 = f32[128,128]{1,0:T(8,128)} custom-call(f32[128,128]{1,0:T(8,128)} %slice.183.d_ref), custom_call_target="tpu_custom_call" | custom-call | flops 12582912 | bytes 131072 | tf_op jit(solution)/shard_map/pallas_call | solution.py:76
  248.3 1.6 fusion.15
  250.6 4.6 %slice_subtract_fusion = f32[896,896]{1,0:T(8,128)S(1)} fusion(f32[1024,1024]{1,0:T(8,128)} %copy-done.8, f32[896,128]{1,0:T(8,128)S(1)} %fusion.15), kind=kOutput, calls=%fused_computation.7 | convolution fusion | flops 1233928192 | bytes 7340032 | tf_op jit(solution)/shard_map/dot_general | solution.py:100
  255.9 13.0 %shard_map.65 = f32[128,128]{1,0:T(8,128)} custom-call(f32[128,128]{1,0:T(8,128)} %slice.187.d_ref), custom_call_target="tpu_custom_call" | custom-call | flops 12582912 | bytes 131072 | tf_op jit(solution)/shard_map/pallas_call | solution.py:76
  268.9 1.3 fusion.17
  270.2 2.0 slice_subtract_fusion.1
  272.2 1.4 copy-done.2
  274.3 13.2 %shard_map.66 = f32[128,128]{1,0:T(8,128)} custom-call(f32[128,128]{1,0:T(8,128)} %slice.192.d_ref), custom_call_target="tpu_custom_call" | custom-call | flops 12582912 | bytes 131072 | tf_op jit(solution)/shard_map/pallas_call | solution.py:76
  287.5 1.4 fusion.19
  288.9 2.9 slice_subtract_fusion.2
  292.4 13.0 %shard_map.67 = f32[128,128]{1,0:T(8,128)} custom-call(f32[128,128]{1,0:T(8,128)} %slice.197.d_ref), custom_call_target="tpu_custom_call" | custom-call | flops 12582912 | bytes 131072 | tf_op jit(solution)/shard_map/pallas_call | solution.py:76
  309.3 13.0 %shard_map.68 = f32[128,128]{1,0:T(8,128)} custom-call(f32[128,128]{1,0:T(8,128)} %slice.202.d_ref), custom_call_target="tpu_custom_call" | custom-call | flops 12582912 | bytes 131072 | tf_op jit(solution)/shard_map/pallas_call | solution.py:76
  323.6 1.7 convolution_subtract_fusion.1
  326.0 13.0 %shard_map.69 = f32[128,128]{1,0:T(8,128)} custom-call(f32[128,128]{1,0:T(8,128)} %slice.207.d_ref), custom_call_target="tpu_custom_call" | custom-call | flops 12582912 | bytes 131072 | tf_op jit(solution)/shard_map/pallas_call | solution.py:76
  341.2 13.2 %shard_map.70 = f32[128,128]{1,0:T(8,128)} custom-call(f32[128,128]{1,0:T(8,128)} %slice.212.d_ref), custom_call_target="tpu_custom_call" | custom-call | flops 12582912 | bytes 131072 | tf_op jit(solution)/shard_map/pallas_call | solution.py:76
  360.6 13.0 %shard_map.71 = f32[128,128]{1,0:T(8,128)} custom-call(f32[128,128]{1,0:T(8,128)} %convolution_subtract_fusion.10.d_ref), custom_call_target="tpu_custom_call" | custom-call | flops 12582912 | bytes 131072 | tf_op jit(solution)/shard_map/pallas_call | solution.py:76
  (90 shorter events, 31.9 us)
Async XLA Ops:
  6.5 158.8 %reduce-scatter.2.cloned.1.call-start = ((), (), s32[]{:S(2)}) async-start(), calls=%async_computation.1 | async-start | bytes 8912896 | tf_op jit(solution)/shard_map/reduce_scatter | solution.py:141
  16.7 2.0 copy-start
  18.7 8.3 %copy-start.16 = (f32[2,8,128]{2,1,0:T(8,128)S(1)}, f32[2,8,128]{2,1,0:T(8,128)}, u32[]{:S(2)}) copy-start(f32[2,8,128]{2,1,0:T(8,128)} %param.10) | copy-start | bytes 24580
  18.9 8.2 %collective-permute-start.1 = (bf16[128,4,512]{2,0,1:T(8,128)(2,1)S(1)}, bf16[128,4,512]{2,0,1:T(8,128)(2,1)S(1)}, u32[]{:S(2)}, u32[]{:S(2)}) collective-permute-start(bf16[128,4,512]{2,0,1:T(8,128)(2,1)S(1)} %get-tuple-element.11), channel_id=1, source_target_pairs={{16,0},{32,16},{48,32},{64,48},{80,64},{96,80},{112,96},{17,1},{33... | collective-permute-start | bytes 1572872 | tf_op jit(solution)/shard_map/ppermute | solution.py:19
  20.2 6.9 %collective-permute-start.3 = (bf16[128,4,512]{2,0,1:T(8,128)(2,1)S(1)}, bf16[128,4,512]{2,0,1:T(8,128)(2,1)S(1)}, u32[]{:S(2)}, u32[]{:S(2)}) collective-permute-start(bf16[128,4,512]{2,0,1:T(8,128)(2,1)S(1)} %get-tuple-element.12), channel_id=1, source_target_pairs={{0,16},{16,32},{32,48},{48,64},{64,80},{80,96},{96,112},{1,17},{17... | collective-permute-start | bytes 1572872 | tf_op jit(solution)/shard_map/ppermute | solution.py:19
  25.2 11.3 %copy-start.1 = (bf16[1024,4,512]{2,0,1:T(8,128)(2,1)S(1)}, bf16[1024,4,512]{2,0,1:T(8,128)(2,1)}, u32[]{:S(2)}) copy-start(bf16[1024,4,512]{2,0,1:T(8,128)(2,1)} %copy-done) | copy-start | bytes 12582916
  29.1 11.3 %collective-permute-start = (bf16[128,4,512]{2,0,1:T(8,128)(2,1)S(1)}, bf16[128,4,512]{2,0,1:T(8,128)(2,1)S(1)}, u32[]{:S(2)}, u32[]{:S(2)}) collective-permute-start(bf16[128,4,512]{2,0,1:T(8,128)(2,1)S(1)} %get-tuple-element.10), channel_id=1, source_target_pairs={{16,0},{32,16},{48,32},{64,48},{80,64},{96,80},{112,96},{17,1},{33... | collective-permute-start | bytes 1572872 | tf_op jit(solution)/shard_map/ppermute | solution.py:19
  30.4 21.5 %collective-permute-start.2 = (bf16[128,4,512]{2,0,1:T(8,128)(2,1)S(1)}, bf16[128,4,512]{2,0,1:T(8,128)(2,1)S(1)}, u32[]{:S(2)}, u32[]{:S(2)}) collective-permute-start(bf16[128,4,512]{2,0,1:T(8,128)(2,1)S(1)} %get-tuple-element.8), channel_id=1, source_target_pairs={{0,16},{16,32},{32,48},{48,64},{64,80},{80,96},{96,112},{1,17},{17... | collective-permute-start | bytes 1572872 | tf_op jit(solution)/shard_map/ppermute | solution.py:19
  74.1 93.0 %copy-start.17 = (s32[8]{0:T(128)S(1)}, s32[8]{0:T(128)}, u32[]{:S(2)}) copy-start(s32[8]{0:T(128)} %param.11) | copy-start | bytes 100
  74.1 150.3 %all-gather.2.cloned.1.call-start = ((), (), s32[]{:S(2)}) async-start(), calls=%async_computation.2 | async-start | bytes 4456448 | tf_op jit(solution)/shard_map/all_gather | solution.py:147
  232.6 2.0 copy-start.8
  249.8 0.8 copy-start.3
  270.2 2.0 copy-start.5
  272.2 1.4 copy-start.2
  291.8 63.8 %copy-start.15 = (f32[128,128]{1,0:T(8,128)S(1)}, f32[128,128]{1,0:T(8,128)}, u32[]{:S(2)}) copy-start(f32[128,128]{1,0:T(8,128)} %shard_map.64) | copy-start | bytes 196612
  291.8 64.0 %copy-start.4 = (f32[896,128]{1,0:T(8,128)S(1)}, f32[896,128]{1,0:T(8,128)}, u32[]{:S(2)}) copy-start(f32[896,128]{1,0:T(8,128)} %copy-done.3) | copy-start | bytes 1376260
  306.6 49.7 %copy-start.14 = (f32[128,128]{1,0:T(8,128)S(1)}, f32[128,128]{1,0:T(8,128)}, u32[]{:S(2)}) copy-start(f32[128,128]{1,0:T(8,128)} %shard_map.65) | copy-start | bytes 196612
  306.6 49.9 %copy-start.6 = (f32[768,128]{1,0:T(8,128)S(1)}, f32[768,128]{1,0:T(8,128)}, u32[]{:S(2)}) copy-start(f32[768,128]{1,0:T(8,128)} %copy-done.5) | copy-start | bytes 1179652
  307.7 1.0 copy-start.7
  308.6 48.4 %copy-start.13 = (f32[128,128]{1,0:T(8,128)S(1)}, f32[128,128]{1,0:T(8,128)}, u32[]{:S(2)}) copy-start(f32[128,128]{1,0:T(8,128)} %shard_map.66) | copy-start | bytes 196612
  308.6 49.0 %copy-start.12 = (f32[128,128]{1,0:T(8,128)S(1)}, f32[128,128]{1,0:T(8,128)}, u32[]{:S(2)}) copy-start(f32[128,128]{1,0:T(8,128)} %shard_map.67) | copy-start | bytes 196612
  323.6 34.7 %copy-start.11 = (f32[128,128]{1,0:T(8,128)S(1)}, f32[128,128]{1,0:T(8,128)}, u32[]{:S(2)}) copy-start(f32[128,128]{1,0:T(8,128)} %shard_map.68) | copy-start | bytes 196612
  339.0 19.8 %copy-start.10 = (f32[128,128]{1,0:T(8,128)S(1)}, f32[128,128]{1,0:T(8,128)}, u32[]{:S(2)}) copy-start(f32[128,128]{1,0:T(8,128)} %shard_map.69) | copy-start | bytes 196612
  354.4 5.8 %copy-start.9 = (f32[128,128]{1,0:T(8,128)S(1)}, f32[128,128]{1,0:T(8,128)}, u32[]{:S(2)}) copy-start(f32[128,128]{1,0:T(8,128)} %shard_map.70) | copy-start | bytes 196612
Sparse Core Ops, SparseCore 0:
  74.3 91.0 reduce-scatter.1
  167.4 56.9 all-gather.1

commit v5 on v4

--- a/solution.py
+++ b/solution.py
@@ -8,6 +8,7 @@
 
 KOUT = 2048
 BLOCK = 128
+CHUNK = 256
 PHASE = 16
 UNROLL = 4
 HI = lax.Precision.HIGHEST
@@ -82,27 +83,43 @@
     )(diag)
 
 
-def cholesky_solve(gram, rhs):
-    n = gram.shape[0]
-    trailing = gram
-    rest = rhs
-    solved = []
-    for start in range(0, n, BLOCK):
-        diag = trailing[:BLOCK, :BLOCK]
-        inverse = factor_inverse(diag)
-        head = dot(inverse, rest[:BLOCK])
-        solved.append(head)
-        if start + BLOCK < n:
-            panel = lax.dot_general(
-                trailing[BLOCK:, :BLOCK], inverse, (((1,), (1,)), ((), ())),
+def bordered_solve(chunks, rhs_blocks, dead_blocks):
+    lead_inverse = None
+    solved = None
+    for k, cols in enumerate(chunks):
+        seen = jnp.concatenate(chunks[: k + 1], 1) if k else cols
+        gram_row = lax.dot_general(
+            cols, seen, (((0,), (0,)), ((), ())), preferred_element_type=jnp.float32
+        )
+        diag = gram_row[:, k * BLOCK:] + jnp.diag(dead_blocks[k])
+        rhs = rhs_blocks[k]
+        if k:
+            row = lax.dot_general(
+                gram_row[:, : k * BLOCK], lead_inverse, (((1,), (1,)), ((), ())),
                 precision=HI, preferred_element_type=jnp.float32,
             )
-            trailing = trailing[BLOCK:, BLOCK:] - lax.dot_general(
-                panel, panel, (((1,), (1,)), ((), ())),
+            diag = diag - lax.dot_general(
+                row, row, (((1,), (1,)), ((), ())),
                 precision=HI, preferred_element_type=jnp.float32,
             )
-            rest = rest[BLOCK:] - dot(panel, head)
-    return jnp.concatenate(solved, 0)
+            rhs = rhs - dot(row, solved)
+        inverse = factor_inverse(diag)
+        head = dot(inverse, rhs)
+        if k == 0:
+            lead_inverse = inverse
+            solved = head
+        else:
+            below = -dot(inverse, dot(row, lead_inverse))
+            width = lead_inverse.shape[0]
+            lead_inverse = jnp.concatenate(
+                [
+                    jnp.concatenate([lead_inverse, jnp.zeros((width, BLOCK), jnp.float32)], 1),
+                    jnp.concatenate([below, inverse], 1),
+                ],
+                0,
+            )
+            solved = jnp.concatenate([solved, head], 0)
+    return solved
 
 
 def per_device(amplitudes, next_site, sector_rows, moves, angles, ranks):
@@ -138,19 +155,19 @@
     padded = lax.dynamic_update_slice_in_dim(padded, new_b[1], starts_b[1], 0)
     block_rows = padded[:rows]
     site_tensor = next_site[0]
-    contracted = lax.psum_scatter(
-        jnp.einsum("prk,lpr->kl", site_tensor, block_rows, preferred_element_type=jnp.float32),
-        "row",
-        scatter_dimension=0,
-        tiled=True,
-    ).astype(jnp.bfloat16)
-    gathered = lax.all_gather(contracted, "row", axis=0, tiled=True)
-    gram_matrix = lax.dot_general(
-        gathered, gathered, (((0,), (0,)), ((), ())), preferred_element_type=jnp.float32
-    )
+    partial = jnp.einsum("prk,lpr->kl", site_tensor, block_rows, preferred_element_type=jnp.float32)
     dead_rows = (row_index >= live_rows).astype(jnp.float32)
-    gram_matrix = gram_matrix + jnp.diag(dead_rows)
-    solved = cholesky_solve(gram_matrix, contracted.astype(jnp.float32).T).T
+    chunks, rhs_blocks, dead_blocks = [], [], []
+    for start in range(0, rows, CHUNK):
+        local = lax.psum_scatter(
+            partial[:, start:start + CHUNK], "row", scatter_dimension=0, tiled=True
+        ).astype(jnp.bfloat16)
+        gathered = lax.all_gather(local, "row", axis=0, tiled=True)
+        for sub in range(0, CHUNK, BLOCK):
+            chunks.append(gathered[:, sub:sub + BLOCK])
+            rhs_blocks.append(local[:, sub:sub + BLOCK].astype(jnp.float32).T)
+            dead_blocks.append(dead_rows[start + sub:start + sub + BLOCK])
+    solved = bordered_solve(chunks, rhs_blocks, dead_blocks).T
     kept_mask = ((row_index >= live_rows - ranks[sector_id]) & (row_index < live_rows)).astype(
         jnp.float32
     )

time: 384 us -> 641 us (1.67); the launches traced: 383 us -> 632 us
  waiting for transfers between devices: 144 us -> 366 us
  matrix products: 50.3 us -> 70.6 us
  other arithmetic: 18.1 us -> 25.2 us
    reduce_scatter x1 -> x4, waiting for transfers between devices: 91 us -> 302 us  [per_device(): lax.psum_scatter(partial[:, start:start + CHUNK], 'row', scatter_dimensio...]
    dot_general x15 -> x27, matrix products: 4.95 us -> 25.4 us  [dot(): return jnp.dot(a, b, precision=HI, preferred_element_type=jnp.float32)]
    all_gather x1 -> x4, waiting for transfers between devices: 53.3 us -> 62.5 us  [per_device(): gathered = lax.all_gather(local, 'row', axis=0, tiled=True)]
    dot_general x15 -> x22, matrix products: 30.8 us -> 32.7 us  [the longest x8 14.9 us: bordered_solve(): lax.dot_general(cols, seen, (((0,), (0,)), ((), ())), preferred_element_t...]
  transfers between devices with their start and end apart: 6 -> 12, of which waited for: 2 -> 7; matrix products, arithmetic and copies ran while one was open for 5% -> 10% of each run, Pallas kernels for 0% -> 12%
where the time goes in v5:
time: 641 us; the launch traced here: 632 us
  waiting for transfers between devices  366 us (57%)
  Pallas kernels  105 us (16%)
  matrix products  70.6 us (11%)
  local copies, waits for them, and re-layouts  32.8 us (5%)
  other arithmetic  25.2 us (4%)
  between operations  19.9 us (3%)
  starting transfers between devices  12.6 us (2%)
    reduce_scatter x4, waiting for transfers between devices, per_device(): lax.psum_scatter(partial[:, start:start + CHUNK], 'row', scatter_dimensio...  302 us
    pallas_call x8, Pallas kernels, factor_inverse(): pl.pallas_call(factor_inverse_kernel, out_shape=jax.ShapeDtypeStruct((n,...  105 us
    all_gather x4, waiting for transfers between devices, per_device(): gathered = lax.all_gather(local, 'row', axis=0, tiled=True)  62.5 us
    dot_general x27, matrix products, dot(): return jnp.dot(a, b, precision=HI, preferred_element_type=jnp.float32)  25.4 us
    dot_general x8, matrix products, bordered_solve(): lax.dot_general(cols, seen, (((0,), (0,)), ((), ())), preferred_element_t...  14.9 us
  transfers between devices with their start and end apart: 12, of which 7 were waited for; matrix products, arithmetic and copies ran while one was open for 10% of the time, Pallas kernels for 12%

profile of v5, /device:TPU:0, one launch (start us, length us, event | category | flops | bytes accessed | tf_op | source)
XLA Modules:
  0.0 632.2 jit_solution(10181684487679319112)
XLA Ops:
  11.7 5.1 copy_select_fusion
  20.1 3.1 collective-permute-start.3
  29.8 6.7 %collective-permute-start.2 = (bf16[128,4,512]{2,0,1:T(8,128)(2,1)S(1)}, bf16[128,4,512]{2,0,1:T(8,128)(2,1)S(1)}, u32[]{:S(2)}, u32[]{:S(2)}) collective-permute-start(bf16[128,4,512]{2,0,1:T(8,128)(2,1)S(1)} %get-tuple-element.8), channel_id=1, source_target_pairs={{0,16},{16,32},{32,48},{48,64},{64,80},{80,96},{96,112},{1,17},{17... | collective-permute-start | bytes 1572872 | tf_op jit(solution)/shard_map/ppermute | solution.py:20
  36.5 2.5 concatenate.109
  40.6 5.6 dynamic_update_slice.12
  46.2 5.5 dynamic_update_slice.13
  51.7 2.1 fusion.57
  53.8 5.6 dynamic_update_slice.15
  59.4 12.5 %fusion.2 = f32[2048,1024]{0,1:T(8,128)S(1)} fusion(bf16[1,4,512,2048]{3,2,1,0:T(8,128)(2,1)} %param.7, bf16[1152,4,512]{2,0,1:T(8,128)(2,1)} %dynamic_update_slice.15), kind=kOutput, calls=%fused_computation.2 | convolution fusion | flops 8589934592 | bytes 20971520 | tf_op jit(solution)/shard_map/prk,lpr->kl/dot_general | solution.py:158
  71.9 3.4 fusion.116
  77.4 78.4 %reduce-scatter.5.cloned.1.call-done = f32[128,256]{0,1:T(8,128)} async-done(((f32[2048,256]{0,1:T(8,128)}), f32[128,256]{0,1:T(8,128)}) %reduce-scatter.5.cloned.1.call-update) | async-done | bytes 131088 | tf_op jit(solution)/shard_map/reduce_scatter | solution.py:162
  157.4 75.7 %reduce-scatter.7.cloned.1.call-done = f32[128,256]{0,1:T(8,128)} async-done(((f32[2048,256]{0,1:T(8,128)}), f32[128,256]{0,1:T(8,128)}) %reduce-scatter.7.cloned.1.call-update) | async-done | bytes 131088 | tf_op jit(solution)/shard_map/reduce_scatter | solution.py:162
  234.7 75.4 %reduce-scatter.9.cloned.1.call-done = f32[128,256]{0,1:T(8,128)} async-done(((f32[2048,256]{0,1:T(8,128)}), f32[128,256]{0,1:T(8,128)}) %reduce-scatter.9.cloned.1.call-update) | async-done | bytes 131088 | tf_op jit(solution)/shard_map/reduce_scatter | solution.py:162
  314.9 72.4 %reduce-scatter.11.cloned.1.call-done = f32[128,256]{0,1:T(8,128)} async-done(((f32[2048,256]{0,1:T(8,128)}), f32[128,256]{0,1:T(8,128)}) %reduce-scatter.11.cloned.1.call-update) | async-done | bytes 131088 | tf_op jit(solution)/shard_map/reduce_scatter | solution.py:162
  388.9 43.0 %all-gather.5.cloned.1.call-done = bf16[2048,256]{0,1:T(8,128)(2,1)} async-done(((bf16[128,256]{0,1:T(8,128)(2,1)}), bf16[2048,256]{0,1:T(8,128)(2,1)}) %all-gather.5.cloned.1.call-update) | async-done | bytes 1048592 | tf_op jit(solution)/shard_map/all_gather | solution.py:165
  432.0 2.2 convolution_add_fusion.d_ref
  434.2 13.2 %shard_map.64 = f32[128,128]{1,0:T(8,128)} custom-call(f32[128,128]{1,0:T(8,128)} %convolution_add_fusion.d_ref), custom_call_target="tpu_custom_call" | custom-call | flops 12582912 | bytes 131072 | tf_op jit(solution)/shard_map/pallas_call | solution.py:77
  452.3 13.0 %shard_map.65 = f32[128,128]{1,0:T(8,128)} custom-call(f32[128,128]{1,0:T(8,128)} %convolution_subtract_fusion.9.d_ref), custom_call_target="tpu_custom_call" | custom-call | flops 12582912 | bytes 131072 | tf_op jit(solution)/shard_map/pallas_call | solution.py:77
  467.3 9.8 %all-gather.7.cloned.1.call-done = bf16[2048,256]{0,1:T(8,128)(2,1)} async-done(((bf16[128,256]{0,1:T(8,128)(2,1)}), bf16[2048,256]{0,1:T(8,128)(2,1)}) %all-gather.7.cloned.1.call-update) | async-done | bytes 1048592 | tf_op jit(solution)/shard_map/all_gather | solution.py:165
  480.5 13.0 %shard_map.66 = f32[128,128]{1,0:T(8,128)} custom-call(f32[128,128]{1,0:T(8,128)} %convolution_subtract_fusion.7.d_ref), custom_call_target="tpu_custom_call" | custom-call | flops 12582912 | bytes 131072 | tf_op jit(solution)/shard_map/pallas_call | solution.py:77
  498.7 13.0 %shard_map.67 = f32[128,128]{1,0:T(8,128)} custom-call(f32[128,128]{1,0:T(8,128)} %convolution_subtract_fusion.13.d_ref), custom_call_target="tpu_custom_call" | custom-call | flops 12582912 | bytes 131072 | tf_op jit(solution)/shard_map/pallas_call | solution.py:77
  512.8 9.6 %all-gather.9.cloned.1.call-done = bf16[2048,256]{0,1:T(8,128)(2,1)} async-done(((bf16[128,256]{0,1:T(8,128)(2,1)}), bf16[2048,256]{0,1:T(8,128)(2,1)}) %all-gather.9.cloned.1.call-update) | async-done | bytes 1048592 | tf_op jit(solution)/shard_map/all_gather | solution.py:165
  523.6 2.2 fusion.33
  528.7 13.2 %shard_map.68 = f32[128,128]{1,0:T(8,128)} custom-call(f32[128,128]{1,0:T(8,128)} %convolution_subtract_fusion.11.d_ref), custom_call_target="tpu_custom_call" | custom-call | flops 12582912 | bytes 131072 | tf_op jit(solution)/shard_map/pallas_call | solution.py:77
  543.2 2.9 fusion.27
  548.9 13.0 %shard_map.69 = f32[128,128]{1,0:T(8,128)} custom-call(f32[128,128]{1,0:T(8,128)} %convolution_subtract_fusion.5.d_ref), custom_call_target="tpu_custom_call" | custom-call | flops 12582912 | bytes 131072 | tf_op jit(solution)/shard_map/pallas_call | solution.py:77
  570.0 2.7 fusion.14
  572.7 2.5 fusion.65
  575.2 2.1 fusion.115
  578.5 13.3 %shard_map.70 = f32[128,128]{1,0:T(8,128)} custom-call(f32[128,128]{1,0:T(8,128)} %convolution_subtract_fusion.3.d_ref), custom_call_target="tpu_custom_call" | custom-call | flops 12582912 | bytes 131072 | tf_op jit(solution)/shard_map/pallas_call | solution.py:77
  604.7 3.1 fusion.22
  609.8 13.0 %shard_map.71 = f32[128,128]{1,0:T(8,128)} custom-call(f32[128,128]{1,0:T(8,128)} %convolution_subtract_fusion.1.d_ref), custom_call_target="tpu_custom_call" | custom-call | flops 12582912 | bytes 131072 | tf_op jit(solution)/shard_map/pallas_call | solution.py:77
  (177 shorter events, 73.4 us)
Async XLA Ops:
  6.5 149.3 %reduce-scatter.5.cloned.1.call-start = ((), (), s32[]{:S(2)}) async-start(), calls=%async_computation.4 | async-start | bytes 2228224 | tf_op jit(solution)/shard_map/reduce_scatter | solution.py:162
  16.8 9.5 %copy-start.38 = (f32[2,8,128]{2,1,0:T(8,128)S(1)}, f32[2,8,128]{2,1,0:T(8,128)}, u32[]{:S(2)}) copy-start(f32[2,8,128]{2,1,0:T(8,128)} %param.10) | copy-start | bytes 24580
  18.8 7.6 %collective-permute-start.1 = (bf16[128,4,512]{2,0,1:T(8,128)(2,1)S(1)}, bf16[128,4,512]{2,0,1:T(8,128)(2,1)S(1)}, u32[]{:S(2)}, u32[]{:S(2)}) collective-permute-start(bf16[128,4,512]{2,0,1:T(8,128)(2,1)S(1)} %get-tuple-element.15), channel_id=1, source_target_pairs={{16,0},{32,16},{48,32},{64,48},{80,64},{96,80},{112,96},{17,1},{33... | collective-permute-start | bytes 1572872 | tf_op jit(solution)/shard_map/ppermute | solution.py:20
  20.1 6.4 %collective-permute-start.3 = (bf16[128,4,512]{2,0,1:T(8,128)(2,1)S(1)}, bf16[128,4,512]{2,0,1:T(8,128)(2,1)S(1)}, u32[]{:S(2)}, u32[]{:S(2)}) collective-permute-start(bf16[128,4,512]{2,0,1:T(8,128)(2,1)S(1)} %get-tuple-element.16), channel_id=1, source_target_pairs={{0,16},{16,32},{32,48},{48,64},{64,80},{80,96},{96,112},{1,17},{17... | collective-permute-start | bytes 1572872 | tf_op jit(solution)/shard_map/ppermute | solution.py:20
  26.5 10.0 %copy-start.1 = (bf16[1024,4,512]{2,0,1:T(8,128)(2,1)S(1)}, bf16[1024,4,512]{2,0,1:T(8,128)(2,1)}, u32[]{:S(2)}) copy-start(bf16[1024,4,512]{2,0,1:T(8,128)(2,1)} %copy-done) | copy-start | bytes 12582916
  28.5 11.7 %collective-permute-start = (bf16[128,4,512]{2,0,1:T(8,128)(2,1)S(1)}, bf16[128,4,512]{2,0,1:T(8,128)(2,1)S(1)}, u32[]{:S(2)}, u32[]{:S(2)}) collective-permute-start(bf16[128,4,512]{2,0,1:T(8,128)(2,1)S(1)} %get-tuple-element.14), channel_id=1, source_target_pairs={{16,0},{32,16},{48,32},{64,48},{80,64},{96,80},{112,96},{17,1},{33... | collective-permute-start | bytes 1572872 | tf_op jit(solution)/shard_map/ppermute | solution.py:20
  29.8 21.8 %collective-permute-start.2 = (bf16[128,4,512]{2,0,1:T(8,128)(2,1)S(1)}, bf16[128,4,512]{2,0,1:T(8,128)(2,1)S(1)}, u32[]{:S(2)}, u32[]{:S(2)}) collective-permute-start(bf16[128,4,512]{2,0,1:T(8,128)(2,1)S(1)} %get-tuple-element.8), channel_id=1, source_target_pairs={{0,16},{16,32},{32,48},{48,64},{64,80},{80,96},{96,112},{1,17},{17... | collective-permute-start | bytes 1572872 | tf_op jit(solution)/shard_map/ppermute | solution.py:20
  75.3 157.8 %reduce-scatter.7.cloned.1.call-start = ((), (), s32[]{:S(2)}) async-start(), calls=%async_computation.6 | async-start | bytes 2228224 | tf_op jit(solution)/shard_map/reduce_scatter | solution.py:162
  76.1 235.7 %copy-start.40 = (s32[8]{0:T(128)S(1)}, s32[8]{0:T(128)}, u32[]{:S(2)}) copy-start(s32[8]{0:T(128)} %param.11) | copy-start | bytes 100
  76.1 234.0 %reduce-scatter.9.cloned.1.call-start = ((), (), s32[]{:S(2)}) async-start(), calls=%async_computation.8 | async-start | bytes 2228224 | tf_op jit(solution)/shard_map/reduce_scatter | solution.py:162
  76.8 310.5 %reduce-scatter.11.cloned.1.call-start = ((), (), s32[]{:S(2)}) async-start(), calls=%async_computation.10 | async-start | bytes 2228224 | tf_op jit(solution)/shard_map/reduce_scatter | solution.py:162
  77.4 354.6 %all-gather.5.cloned.1.call-start = ((), (), s32[]{:S(2)}) async-start(), calls=%async_computation.5 | async-start | bytes 1114112 | tf_op jit(solution)/shard_map/all_gather | solution.py:165
  157.4 319.8 %all-gather.7.cloned.1.call-start = ((), (), s32[]{:S(2)}) async-start(), calls=%async_computation.7 | async-start | bytes 1114112 | tf_op jit(solution)/shard_map/all_gather | solution.py:165
  234.7 287.8 %all-gather.9.cloned.1.call-start = ((), (), s32[]{:S(2)}) async-start(), calls=%async_computation.9 | async-start | bytes 1114112 | tf_op jit(solution)/shard_map/all_gather | solution.py:165
  311.7 257.2 %all-gather.11.cloned.1.call-start = ((), (), s32[]{:S(2)}) async-start(), calls=%async_computation.11 | async-start | bytes 1114112 | tf_op jit(solution)/shard_map/all_gather | solution.py:165
  432.0 46.3 %copy-start.3 = (bf16[2048,256]{0,1:T(8,128)(2,1)S(1)}, bf16[2048,256]{0,1:T(8,128)(2,1)}, u32[]{:S(2)}) copy-start(bf16[2048,256]{0,1:T(8,128)(2,1)} %all-gather.5.cloned.1.call-done) | copy-start | bytes 3145732
  447.4 19.1 %copy-start.6 = (f32[128,128]{1,0:T(8,128)S(1)}, f32[128,128]{1,0:T(8,128)}, u32[]{:S(2)}) copy-start(f32[128,128]{1,0:T(8,128)} %shard_map.64) | copy-start | bytes 196612
  465.3 13.5 %copy-start.16 = (f32[128,128]{1,0:T(8,128)S(1)}, f32[128,128]{1,0:T(8,128)}, u32[]{:S(2)}) copy-start(f32[128,128]{1,0:T(8,128)} %shard_map.65) | copy-start | bytes 196612
  478.9 16.7 %copy-start.34 = (bf16[2048,256]{0,1:T(8,128)(2,1)S(1)}, bf16[2048,256]{0,1:T(8,128)(2,1)}, u32[]{:S(2)}) copy-start(bf16[2048,256]{0,1:T(8,128)(2,1)} %all-gather.7.cloned.1.call-done) | copy-start | bytes 3145732
  479.3 14.2 %copy-start.11 = (f32[128,256]{1,0:T(8,128)}, f32[128,256]{1,0:T(8,128)S(1)}, u32[]{:S(2)}) copy-start(f32[128,256]{1,0:T(8,128)S(1)} %fusion.86) | copy-start | bytes 393220
  575.2 16.6 %copy-start.8 = (f32[128,128]{1,0:T(8,128)S(1)}, f32[128,128]{1,0:T(8,128)}, u32[]{:S(2)}) copy-start(f32[128,128]{1,0:T(8,128)} %get-tuple-element.66) | copy-start | bytes 196612
  575.2 16.6 %copy-start.31 = (bf16[128,256]{0,1:T(8,128)(2,1)S(1)}, bf16[128,256]{0,1:T(8,128)(2,1)}, u32[]{:S(2)}) copy-start(bf16[128,256]{0,1:T(8,128)(2,1)} %convert_element_type.82) | copy-start | bytes 196612
  575.2 16.8 %copy-start.17 = (f32[128,128]{1,0:T(8,128)S(1)}, f32[128,128]{1,0:T(8,128)}, u32[]{:S(2)}) copy-start(f32[128,128]{1,0:T(8,128)} %shard_map.65) | copy-start | bytes 196612
  575.2 17.7 %copy-start.12 = (f32[128,256]{1,0:T(8,128)S(1)}, f32[128,256]{1,0:T(8,128)}, u32[]{:S(2)}) copy-start(f32[128,256]{1,0:T(8,128)} %copy-done.11) | copy-start | bytes 393220
  575.2 18.7 %copy-start.19 = (f32[128,128]{1,0:T(8,128)S(1)}, f32[128,128]{1,0:T(8,128)}, u32[]{:S(2)}) copy-start(f32[128,128]{1,0:T(8,128)} %shard_map.66) | copy-start | bytes 196612
  577.4 19.0 %copy-start.25 = (f32[128,128]{1,0:T(8,128)S(1)}, f32[128,128]{1,0:T(8,128)}, u32[]{:S(2)}) copy-start(f32[128,128]{1,0:T(8,128)} %shard_map.67) | copy-start | bytes 196612
  577.4 19.9 %copy-start.29 = (bf16[128,256]{0,1:T(8,128)(2,1)S(1)}, bf16[128,256]{0,1:T(8,128)(2,1)}, u32[]{:S(2)}) copy-start(bf16[128,256]{0,1:T(8,128)(2,1)} %convert_element_type.85) | copy-start | bytes 196612
  577.4 20.3 %copy-start.23 = (f32[128,128]{1,0:T(8,128)S(1)}, f32[128,128]{1,0:T(8,128)}, u32[]{:S(2)}) copy-start(f32[128,128]{1,0:T(8,128)} %shard_map.68) | copy-start | bytes 196612
  577.4 22.7 %copy-start.15 = (f32[128,128]{1,0:T(8,128)S(1)}, f32[128,128]{1,0:T(8,128)}, u32[]{:S(2)}) copy-start(f32[128,128]{1,0:T(8,128)} %shard_map.69) | copy-start | bytes 196612
  577.4 23.6 %copy-start.28 = (bf16[128,256]{0,1:T(8,128)(2,1)S(1)}, bf16[128,256]{0,1:T(8,128)(2,1)}, u32[]{:S(2)}) copy-start(bf16[128,256]{0,1:T(8,128)(2,1)} %convert_element_type.86) | copy-start | bytes 196612
  592.0 10.5 %copy-start.32 = (f32[128,128]{1,0:T(8,128)S(1)}, f32[128,128]{1,0:T(8,128)}, u32[]{:S(2)}) copy-start(f32[128,128]{1,0:T(8,128)} %shard_map.70) | copy-start | bytes 196612
  592.0 10.5 %copy-start.33 = (f32[128,768]{1,0:T(8,128)S(1)}, f32[128,768]{1,0:T(8,128)}, u32[]{:S(2)}) copy-start(f32[128,768]{1,0:T(8,128)} %fusion.115) | copy-start | bytes 1179652
  (21 other events, 77.5 us)
Sparse Core Ops, SparseCore 0:
  75.4 80.3 reduce-scatter.4
  159.4 73.6 reduce-scatter.6
  236.4 73.6 reduce-scatter.8
  313.6 73.7 reduce-scatter.10
  389.3 42.6 all-gather.4
  433.9 43.1 all-gather.6
  479.3 43.1 all-gather.8
  524.6 43.4 all-gather.10

commit v6 on v4

--- a/solution.py
+++ b/solution.py
@@ -4,6 +4,7 @@
 import jax.numpy as jnp
 from jax import lax
 from jax.experimental import pallas as pl
+from jax.experimental.pallas import tpu as pltpu
 from jax.sharding import PartitionSpec as P
 
 KOUT = 2048
@@ -36,13 +37,13 @@
     return jnp.dot(a, b, precision=HI, preferred_element_type=jnp.float32)
 
 
-def factor_inverse_kernel(d_ref, o_ref):
-    n = d_ref.shape[0]
-    a = d_ref[...]
+def block_inverse(a):
+    n = a.shape[0]
     rows_n = lax.broadcasted_iota(jnp.int32, (n, n), 0)
     lanes_n = lax.broadcasted_iota(jnp.int32, (n, n), 1)
     w = (rows_n == lanes_n).astype(jnp.float32)
     diag = jnp.sum(jnp.where(rows_n == lanes_n, a, 0.0), axis=0, keepdims=True)
+    done = []
     for first in range(0, n, PHASE):
         m = n - first
         lane = lax.broadcasted_iota(jnp.int32, (m, n), 1)
@@ -66,43 +67,40 @@
             return a, w, diag
 
         a, w, diag = lax.fori_loop(0, PHASE, body, (a, w, diag), unroll=UNROLL)
-        o_ref[first:first + PHASE, :] = w[:PHASE]
+        done.append(w[:PHASE])
         a = a[PHASE:]
         w = w[PHASE:]
+    return jnp.concatenate(done, 0)
 
 
-def factor_inverse(diag):
-    n = diag.shape[0]
-    return pl.pallas_call(
-        factor_inverse_kernel,
-        out_shape=jax.ShapeDtypeStruct((n, n), jnp.float32),
-        cost_estimate=pl.CostEstimate(
-            flops=6 * n * n * n, transcendentals=n, bytes_accessed=8 * n * n
-        ),
-    )(diag)
+def mm(a, b, transpose_b=False):
+    dims = (((1,), (1 if transpose_b else 0,)), ((), ()))
+    return lax.dot_general(a, b, dims, precision=HI, preferred_element_type=jnp.float32)
+
+
+def solve_kernel(g_ref, b_ref, x_ref, t_ref, r_ref):
+    n = g_ref.shape[0]
+    t_ref[...] = g_ref[...]
+    r_ref[...] = b_ref[...]
+    for start in range(0, n, BLOCK):
+        end = start + BLOCK
+        inverse = block_inverse(t_ref[start:end, start:end])
+        head = mm(inverse, r_ref[start:end, :])
+        x_ref[start:end, :] = head
+        if end < n:
+            panel = mm(t_ref[end:, start:end], inverse, transpose_b=True)
+            t_ref[end:, end:] = t_ref[end:, end:] - mm(panel, panel, transpose_b=True)
+            r_ref[end:, :] = r_ref[end:, :] - mm(panel, head)
 
 
 def cholesky_solve(gram, rhs):
-    n = gram.shape[0]
-    trailing = gram
-    rest = rhs
-    solved = []
-    for start in range(0, n, BLOCK):
-        diag = trailing[:BLOCK, :BLOCK]
-        inverse = factor_inverse(diag)
-        head = dot(inverse, rest[:BLOCK])
-        solved.append(head)
-        if start + BLOCK < n:
-            panel = lax.dot_general(
-                trailing[BLOCK:, :BLOCK], inverse, (((1,), (1,)), ((), ())),
-                precision=HI, preferred_element_type=jnp.float32,
-            )
-            trailing = trailing[BLOCK:, BLOCK:] - lax.dot_general(
-                panel, panel, (((1,), (1,)), ((), ())),
-                precision=HI, preferred_element_type=jnp.float32,
-            )
-            rest = rest[BLOCK:] - dot(panel, head)
-    return jnp.concatenate(solved, 0)
+    n, m = rhs.shape
+    return pl.pallas_call(
+        solve_kernel,
+        out_shape=jax.ShapeDtypeStruct((n, m), jnp.float32),
+        scratch_shapes=[pltpu.VMEM((n, n), jnp.float32), pltpu.VMEM((n, m), jnp.float32)],
+        compiler_params=pltpu.CompilerParams(vmem_limit_bytes=48 * 1024 * 1024),
+    )(gram, rhs)
 
 
 def per_device(amplitudes, next_site, sector_rows, moves, angles, ranks):

time: 384 us -> 348 us (0.906)
  matrix products: 50.3 us -> 22.7 us
  local copies, waits for them, and re-layouts: 34.4 us -> 24.9 us
    dot_general x29 -> x0, matrix products: 27.5 us -> none  [the longest x7 13.5 us: cholesky_solve(): lax.dot_general(panel, panel, (((1,), (1,)), ((), ())), precision=HI, pre...]
    unnamed x36 -> x8, local copies, waits for them, and re-layouts: 7.15 us -> 1.96 us
    slice x7 -> x0, local copies, waits for them, and re-layouts: 4.45 us -> none  [cholesky_solve(): diag = trailing[:BLOCK, :BLOCK]]
    pallas_call x8 -> x1, Pallas kernels: 104 us -> 107 us  [cholesky_solve(): pl.pallas_call(solve_kernel, out_shape=jax.ShapeDtypeStruct((n, m), jnp.f...]
where the time goes in v6:
time: 348 us
  waiting for transfers between devices  145 us (42%)
  Pallas kernels  107 us (31%)
  local copies, waits for them, and re-layouts  24.9 us (7%)
  matrix products  22.7 us (7%)
  between operations  18.7 us (5%)
  other arithmetic  17.1 us (5%)
  starting transfers between devices  11.9 us (3%)
    pallas_call x1, Pallas kernels, cholesky_solve(): pl.pallas_call(solve_kernel, out_shape=jax.ShapeDtypeStruct((n, m), jnp.f...  107 us
    reduce_scatter x1, waiting for transfers between devices, per_device(): lax.psum_scatter(jnp.einsum('prk,lpr->kl', site_tensor, block_rows, prefe...  90.8 us
    all_gather x1, waiting for transfers between devices, per_device(): gathered = lax.all_gather(contracted, 'row', axis=0, tiled=True)  54.1 us
    dot_general x1, matrix products, per_device(): jnp.einsum('prk,lpr->kl', site_tensor, block_rows, preferred_element_type...  14.6 us
    ppermute x4, starting transfers between devices, shifted(): return lax.ppermute(x, axis, pairs)  11.9 us
    dot_general x1, matrix products, per_device(): lax.dot_general(gathered, gathered, (((0,), (0,)), ((), ())), preferred_e...  8.09 us
  transfers between devices with their start and end apart: 6, of which 2 were waited for; matrix products, arithmetic and copies ran while one was open for 5% of the time, Pallas kernels for 0%

profile of v6, /device:TPU:0, one launch (start us, length us, event | category | flops | bytes accessed | tf_op | source)
XLA Modules:
  0.0 347.6 jit_solution(10161608413286278855)
XLA Ops:
  6.5 1.3 dynamic_slice.36
  7.8 0.6 iota_compare_fusion.3
  8.5 0.8 fusion.19
  9.3 0.6 fusion.22
  11.8 5.1 %copy_select_fusion = bf16[1024,4,512]{2,0,1:T(8,128)(2,1)S(1)} fusion(bf16[1024,4,512]{2,1,0:T(4,128)(2,1)} %param.6, pred[1024]{0:T(1024)(128)(4,1)S(1)} %iota_compare_fusion.3), kind=kLoop, calls=%fused_computation.4 | loop fusion | flops 2097152 | bytes 8389632 | tf_op jit(solution)/shard_map/jit(_where)/select_n | solution.py:115
  16.9 1.9 copy-done
  19.0 1.3 collective-permute-start.1
  20.3 3.1 collective-permute-start.3
  25.4 0.8 iota_compare_fusion.6
  26.2 0.8 iota_compare_fusion.4
  27.1 2.0 fusion.9
  29.1 1.3 collective-permute-start
  30.4 6.2 %collective-permute-start.2 = (bf16[128,4,512]{2,0,1:T(8,128)(2,1)S(1)}, bf16[128,4,512]{2,0,1:T(8,128)(2,1)S(1)}, u32[]{:S(2)}, u32[]{:S(2)}) collective-permute-start(bf16[128,4,512]{2,0,1:T(8,128)(2,1)S(1)} %get-tuple-element.10), channel_id=1, source_target_pairs={{0,16},{16,32},{32,48},{48,64},{64,80},{80,96},{96,112},{1,17},{17... | collective-permute-start | bytes 1572872 | tf_op jit(solution)/shard_map/ppermute | solution.py:20
  36.6 2.6 concatenate.3
  39.2 0.6 iota_compare_fusion.7
  39.8 0.7 iota_compare_fusion.5
  40.5 0.3 fusion.7
  40.8 5.6 %dynamic_update_slice.12 = bf16[1152,4,512]{2,0,1:T(8,128)(2,1)} dynamic-update-slice(bf16[1152,4,512]{2,0,1:T(8,128)(2,1)} %concatenate.3, bf16[128,4,512]{2,0,1:T(8,128)(2,1)S(1)} %fusion.7, s32[]{:T(128)S(6)} %select_n.55, s32[]{:T(128)} %constant.22.clone.1, s32[]{:T(128)} %constant.22.clone.1) | dynamic-update-slice | bytes 1048580 | tf_op jit(solution)/shard_map/dynamic_update_slice | solution.py:133
  46.4 5.6 %dynamic_update_slice.13 = bf16[1152,4,512]{2,0,1:T(8,128)(2,1)} dynamic-update-slice(bf16[1152,4,512]{2,0,1:T(8,128)(2,1)} %dynamic_update_slice.12, bf16[128,4,512]{2,0,1:T(8,128)(2,1)S(1)} %get-tuple-element.9, s32[]{:T(128)S(6)} %select_n.60, s32[]{:T(128)} %constant.22.clone.1, s32[]{:T(128)} %constant.22.clone.1) | dynamic-update-slice | bytes 1048580 | tf_op jit(solution)/shard_map/dynamic_update_slice | solution.py:134
  52.0 2.1 fusion.14
  54.1 5.6 %dynamic_update_slice.15 = bf16[1152,4,512]{2,0,1:T(8,128)(2,1)} dynamic-update-slice(bf16[1152,4,512]{2,0,1:T(8,128)(2,1)} %fusion.14, bf16[128,4,512]{2,0,1:T(8,128)(2,1)S(1)} %get-tuple-element.11, s32[]{:T(128)S(6)} %select_n.58, s32[]{:T(128)} %constant.22.clone.1, s32[]{:T(128)} %constant.22.clone.1) | dynamic-update-slice | bytes 1048580 | tf_op jit(solution)/shard_map/dynamic_update_slice | solution.py:136
  59.7 14.6 %fusion.2 = f32[2048,1024]{0,1:T(8,128)} fusion(bf16[1,4,512,2048]{3,2,1,0:T(8,128)(2,1)} %param.7, bf16[1152,4,512]{2,0,1:T(8,128)(2,1)} %dynamic_update_slice.15), kind=kOutput, calls=%fused_computation.2 | convolution fusion | flops 8589934592 | bytes 20971520 | tf_op jit(solution)/shard_map/prk,lpr->kl/dot_general | solution.py:140
  74.3 90.8 %reduce-scatter.2.cloned.1.call-done = f32[128,1024]{0,1:T(8,128)} async-done(((f32[2048,1024]{0,1:T(8,128)}), f32[128,1024]{0,1:T(8,128)}) %reduce-scatter.2.cloned.1.call-update) | async-done | bytes 524304 | tf_op jit(solution)/shard_map/reduce_scatter | solution.py:139
  165.2 1.8 convert_bitcast_fusion
  167.0 0.6 dynamic_slice.47
  168.9 0.6 fusion.16
  169.5 0.6 fusion.18
  170.1 54.1 %all-gather.2.cloned.1.call-done = bf16[2048,1024]{0,1:T(8,128)(2,1)} async-done(((bf16[128,1024]{0,1:T(8,128)(2,1)}), bf16[2048,1024]{0,1:T(8,128)(2,1)}) %all-gather.2.cloned.1.call-update) | async-done | bytes 4194320 | tf_op jit(solution)/shard_map/all_gather | solution.py:145
  224.3 8.1 %select_add_fusion.g_ref = f32[1024,1024]{1,0:T(8,128)S(1)} fusion(f32[1024]{0:T(1024)S(1)} %fusion.16, bf16[2048,1024]{0,1:T(8,128)(2,1)} %all-gather.2.cloned.1.call-done), kind=kOutput, calls=%fused_computation.5 | convolution fusion | flops 4298113024 | bytes 8392704 | tf_op jit(solution)/shard_map/dot_general | solution.py:146
  232.4 107.3 %shard_map.64 = f32[1024,128]{1,0:T(8,128)S(1)} custom-call(f32[1024,1024]{1,0:T(8,128)S(1)} %select_add_fusion.g_ref, f32[1024,128]{1,0:T(8,128)S(1)} %get-tuple-element.5.b_ref), custom_call_target="tpu_custom_call" | custom-call | tf_op jit(solution)/shard_map/pallas_call | solution.py:98
  339.7 0.2 fusion.15
  339.9 0.9 copy.8
  (18 shorter events, 0.4 us)
Async XLA Ops:
  6.5 158.6 %reduce-scatter.2.cloned.1.call-start = ((), (), s32[]{:S(2)}) async-start(), calls=%async_computation.1 | async-start | bytes 8912896 | tf_op jit(solution)/shard_map/reduce_scatter | solution.py:139
  16.9 2.0 copy-start
  18.8 8.1 %copy-start.2 = (f32[2,8,128]{2,1,0:T(8,128)S(1)}, f32[2,8,128]{2,1,0:T(8,128)}, u32[]{:S(2)}) copy-start(f32[2,8,128]{2,1,0:T(8,128)} %param.10) | copy-start | bytes 24580
  19.0 8.1 %collective-permute-start.1 = (bf16[128,4,512]{2,0,1:T(8,128)(2,1)S(1)}, bf16[128,4,512]{2,0,1:T(8,128)(2,1)S(1)}, u32[]{:S(2)}, u32[]{:S(2)}) collective-permute-start(bf16[128,4,512]{2,0,1:T(8,128)(2,1)S(1)} %get-tuple-element.13), channel_id=1, source_target_pairs={{16,0},{32,16},{48,32},{64,48},{80,64},{96,80},{112,96},{17,1},{33... | collective-permute-start | bytes 1572872 | tf_op jit(solution)/shard_map/ppermute | solution.py:20
  20.3 6.8 %collective-permute-start.3 = (bf16[128,4,512]{2,0,1:T(8,128)(2,1)S(1)}, bf16[128,4,512]{2,0,1:T(8,128)(2,1)S(1)}, u32[]{:S(2)}, u32[]{:S(2)}) collective-permute-start(bf16[128,4,512]{2,0,1:T(8,128)(2,1)S(1)} %get-tuple-element.14), channel_id=1, source_target_pairs={{0,16},{16,32},{32,48},{48,64},{64,80},{80,96},{96,112},{1,17},{17... | collective-permute-start | bytes 1572872 | tf_op jit(solution)/shard_map/ppermute | solution.py:20
  25.4 11.3 %copy-start.1 = (bf16[1024,4,512]{2,0,1:T(8,128)(2,1)S(1)}, bf16[1024,4,512]{2,0,1:T(8,128)(2,1)}, u32[]{:S(2)}) copy-start(bf16[1024,4,512]{2,0,1:T(8,128)(2,1)} %copy-done) | copy-start | bytes 12582916
  29.1 11.4 %collective-permute-start = (bf16[128,4,512]{2,0,1:T(8,128)(2,1)S(1)}, bf16[128,4,512]{2,0,1:T(8,128)(2,1)S(1)}, u32[]{:S(2)}, u32[]{:S(2)}) collective-permute-start(bf16[128,4,512]{2,0,1:T(8,128)(2,1)S(1)} %get-tuple-element.12), channel_id=1, source_target_pairs={{16,0},{32,16},{48,32},{64,48},{80,64},{96,80},{112,96},{17,1},{33... | collective-permute-start | bytes 1572872 | tf_op jit(solution)/shard_map/ppermute | solution.py:20
  30.4 21.6 %collective-permute-start.2 = (bf16[128,4,512]{2,0,1:T(8,128)(2,1)S(1)}, bf16[128,4,512]{2,0,1:T(8,128)(2,1)S(1)}, u32[]{:S(2)}, u32[]{:S(2)}) collective-permute-start(bf16[128,4,512]{2,0,1:T(8,128)(2,1)S(1)} %get-tuple-element.10), channel_id=1, source_target_pairs={{0,16},{16,32},{32,48},{48,64},{64,80},{80,96},{96,112},{1,17},{17... | collective-permute-start | bytes 1572872 | tf_op jit(solution)/shard_map/ppermute | solution.py:20
  74.3 92.7 %copy-start.3 = (s32[8]{0:T(128)S(1)}, s32[8]{0:T(128)}, u32[]{:S(2)}) copy-start(s32[8]{0:T(128)} %param.11) | copy-start | bytes 100
  74.3 150.0 %all-gather.2.cloned.1.call-start = ((), (), s32[]{:S(2)}) async-start(), calls=%async_computation.2 | async-start | bytes 4456448 | tf_op jit(solution)/shard_map/all_gather | solution.py:145
Sparse Core Ops, SparseCore 0:
  74.4 90.7 reduce-scatter.1
  167.3 56.9 all-gather.1

commit v7 on v6

--- a/solution.py
+++ b/solution.py
@@ -120,8 +120,8 @@
     starts_b = [jnp.int32(0), count_prev[0]]
     own_a = [lax.dynamic_slice_in_dim(padded, s, move_rows, 0) for s in starts_a]
     own_b = [lax.dynamic_slice_in_dim(padded, s, move_rows, 0) for s in starts_b]
-    from_below = [shifted(w, "sector", 1) for w in own_a]
-    from_above = [shifted(w, "sector", -1) for w in own_b]
+    from_below = shifted(jnp.stack(own_a), "sector", 1)
+    from_above = shifted(jnp.stack(own_b), "sector", -1)
     new_a = [
         rotated_window(own_a[g], from_above[g], angles[g][sector_id], count_here[g], -1)
         for g in range(2)

time: 348 us -> 342 us (0.983)
  starting transfers between devices: 11.9 us -> 4.43 us
    ppermute x4 -> x2, starting transfers between devices: 11.9 us -> 4.39 us  [shifted(): return lax.ppermute(x, axis, pairs)]
  transfers between devices with their start and end apart: 6 -> 4, of which waited for: 2 -> 2; matrix products, arithmetic and copies ran while one was open for 5% -> 6% of each run, Pallas kernels for 0% -> 0%
where the time goes in v7:
time: 342 us; the launch traced here: 341 us
  waiting for transfers between devices  148 us (43%)
  Pallas kernels  107 us (31%)
  local copies, waits for them, and re-layouts  23.4 us (7%)
  matrix products  22.5 us (7%)
  between operations  18.6 us (5%)
  other arithmetic  17 us (5%)
  starting transfers between devices  4.43 us (1%)
    pallas_call x1, Pallas kernels, cholesky_solve(): pl.pallas_call(solve_kernel, out_shape=jax.ShapeDtypeStruct((n, m), jnp.f...  107 us
    reduce_scatter x1, waiting for transfers between devices, per_device(): lax.psum_scatter(jnp.einsum('prk,lpr->kl', site_tensor, block_rows, prefe...  93.9 us
    all_gather x1, waiting for transfers between devices, per_device(): gathered = lax.all_gather(contracted, 'row', axis=0, tiled=True)  54.1 us
    dot_general x1, matrix products, per_device(): jnp.einsum('prk,lpr->kl', site_tensor, block_rows, preferred_element_type...  14.4 us
    dot_general x1, matrix products, per_device(): lax.dot_general(gathered, gathered, (((0,), (0,)), ((), ())), preferred_e...  8.09 us
  transfers between devices with their start and end apart: 4, of which 2 were waited for; matrix products, arithmetic and copies ran while one was open for 6% of the time, Pallas kernels for 0%

profile of v7, /device:TPU:0, one launch (start us, length us, event | category | flops | bytes accessed | tf_op | source)
XLA Modules:
  0.0 341.3 jit_solution(16211083779892781364)
XLA Ops:
  6.5 1.3 dynamic_slice.36
  7.8 0.8 constant_dynamic-slice_fusion.5
  8.7 0.6 fusion.21
  12.4 0.7 iota_compare_fusion.3
  13.7 5.1 %copy_select_fusion = bf16[1024,4,512]{2,0,1:T(8,128)(2,1)S(1)} fusion(bf16[1024,4,512]{2,1,0:T(4,128)(2,1)} %param.6, pred[1024]{0:T(1024)(128)(4,1)S(1)} %iota_compare_fusion.3), kind=kLoop, calls=%fused_computation.4 | loop fusion | flops 2097152 | bytes 8389632 | tf_op jit(solution)/shard_map/jit(_where)/select_n | solution.py:115
  18.8 0.7 dynamic-slice_bitcast_fusion
  19.5 0.1 pad_maximum_fusion
  19.6 1.3 collective-permute-start
  20.9 0.1 pad_maximum_fusion.1
  21.0 3.1 collective-permute-start.1
  24.1 2.6 concatenate.3
  26.7 0.6 iota_compare_fusion.6
  27.3 0.7 iota_compare_fusion.7
  28.0 0.6 iota_compare_fusion.5
  28.6 0.7 iota_compare_fusion.4
  29.4 0.8 fusion.9
  30.2 5.6 %dynamic_update_slice.12 = bf16[1152,4,512]{2,0,1:T(8,128)(2,1)} dynamic-update-slice(bf16[1152,4,512]{2,0,1:T(8,128)(2,1)} %concatenate.3, bf16[128,4,512]{2,0,1:T(8,128)(2,1)S(1)} %get-tuple-element.8, s32[]{:T(128)S(6)} %select_n.55, s32[]{:T(128)} %constant.22.clone.1, s32[]{:T(128)} %constant.22.clone.1) | dynamic-update-slice | bytes 1048580 | tf_op jit(solution)/shard_map/dynamic_update_slice | solution.py:133
  35.8 5.6 %dynamic_update_slice.13 = bf16[1152,4,512]{2,0,1:T(8,128)(2,1)} dynamic-update-slice(bf16[1152,4,512]{2,0,1:T(8,128)(2,1)} %dynamic_update_slice.12, bf16[128,4,512]{2,0,1:T(8,128)(2,1)S(1)} %get-tuple-element.7, s32[]{:T(128)S(6)} %select_n.60, s32[]{:T(128)} %constant.22.clone.1, s32[]{:T(128)} %constant.22.clone.1) | dynamic-update-slice | bytes 1048580 | tf_op jit(solution)/shard_map/dynamic_update_slice | solution.py:134
  41.3 1.4 fusion.13
  42.7 2.1 fusion.14
  44.9 5.5 %dynamic_update_slice.15 = bf16[1152,4,512]{2,0,1:T(8,128)(2,1)} dynamic-update-slice(bf16[1152,4,512]{2,0,1:T(8,128)(2,1)} %fusion.14, bf16[128,4,512]{2,0,1:T(8,128)(2,1)S(1)} %fusion.13, s32[]{:T(128)S(6)} %select_n.58, s32[]{:T(128)} %constant.22.clone.1, s32[]{:T(128)} %constant.22.clone.1) | dynamic-update-slice | bytes 1048580 | tf_op jit(solution)/shard_map/dynamic_update_slice | solution.py:136
  50.4 14.4 %fusion.2 = f32[2048,1024]{0,1:T(8,128)} fusion(bf16[1,4,512,2048]{3,2,1,0:T(8,128)(2,1)} %param.7, bf16[1152,4,512]{2,0,1:T(8,128)(2,1)} %dynamic_update_slice.15), kind=kOutput, calls=%fused_computation.2 | convolution fusion | flops 8589934592 | bytes 20971520 | tf_op jit(solution)/shard_map/prk,lpr->kl/dot_general | solution.py:140
  64.9 93.9 %reduce-scatter.2.cloned.1.call-done = f32[128,1024]{0,1:T(8,128)} async-done(((f32[2048,1024]{0,1:T(8,128)}), f32[128,1024]{0,1:T(8,128)}) %reduce-scatter.2.cloned.1.call-update) | async-done | bytes 524304 | tf_op jit(solution)/shard_map/reduce_scatter | solution.py:139
  158.8 1.8 convert_bitcast_fusion
  160.6 0.6 dynamic_slice.47
  162.5 0.7 fusion.16
  163.2 0.7 fusion.18
  163.9 54.1 %all-gather.2.cloned.1.call-done = bf16[2048,1024]{0,1:T(8,128)(2,1)} async-done(((bf16[128,1024]{0,1:T(8,128)(2,1)}), bf16[2048,1024]{0,1:T(8,128)(2,1)}) %all-gather.2.cloned.1.call-update) | async-done | bytes 4194320 | tf_op jit(solution)/shard_map/all_gather | solution.py:145
  218.0 8.1 %select_add_fusion.g_ref = f32[1024,1024]{1,0:T(8,128)S(1)} fusion(f32[1024]{0:T(1024)S(1)} %fusion.16, bf16[2048,1024]{0,1:T(8,128)(2,1)} %all-gather.2.cloned.1.call-done), kind=kOutput, calls=%fused_computation.5 | convolution fusion | flops 4298113024 | bytes 8392704 | tf_op jit(solution)/shard_map/dot_general | solution.py:146
  226.1 107.3 %shard_map.64 = f32[1024,128]{1,0:T(8,128)S(1)} custom-call(f32[1024,1024]{1,0:T(8,128)S(1)} %select_add_fusion.g_ref, f32[1024,128]{1,0:T(8,128)S(1)} %get-tuple-element.5.b_ref), custom_call_target="tpu_custom_call" | custom-call | tf_op jit(solution)/shard_map/pallas_call | solution.py:98
  333.4 0.2 fusion.15
  333.6 0.9 copy.8
  (14 shorter events, 0.2 us)
Async XLA Ops:
  6.5 152.3 %reduce-scatter.2.cloned.1.call-start = ((), (), s32[]{:S(2)}) async-start(), calls=%async_computation.1 | async-start | bytes 8912896 | tf_op jit(solution)/shard_map/reduce_scatter | solution.py:139
  18.8 10.6 %copy-start = (bf16[1024,4,512]{2,0,1:T(8,128)(2,1)}, bf16[1024,4,512]{2,0,1:T(8,128)(2,1)S(1)}, u32[]{:S(2)}) copy-start(bf16[1024,4,512]{2,0,1:T(8,128)(2,1)S(1)} %copy_select_fusion) | copy-start | bytes 12582916
  19.6 9.8 %collective-permute-start = (bf16[2,128,4,512]{3,1,2,0:T(8,128)(2,1)S(1)}, bf16[2,128,4,512]{3,1,2,0:T(8,128)(2,1)S(1)}, u32[]{:S(2)}, u32[]{:S(2)}) collective-permute-start(bf16[2,128,4,512]{3,1,2,0:T(8,128)(2,1)S(1)} %pad_maximum_fusion), channel_id=1, source_target_pairs={{16,0},{32,16},{48,32},{64,48},{80,64},{96,80},{112,96},{17,1},{33... | collective-permute-start | bytes 3145736 | tf_op jit(solution)/shard_map/ppermute | solution.py:20
  21.0 8.3 %copy-start.1 = (f32[2,8,128]{2,1,0:T(8,128)S(1)}, f32[2,8,128]{2,1,0:T(8,128)}, u32[]{:S(2)}) copy-start(f32[2,8,128]{2,1,0:T(8,128)} %param.10) | copy-start | bytes 24580
  21.0 20.3 %collective-permute-start.1 = (bf16[2,128,4,512]{3,1,2,0:T(8,128)(2,1)S(1)}, bf16[2,128,4,512]{3,1,2,0:T(8,128)(2,1)S(1)}, u32[]{:S(2)}, u32[]{:S(2)}) collective-permute-start(bf16[2,128,4,512]{3,1,2,0:T(8,128)(2,1)S(1)} %pad_maximum_fusion.1), channel_id=1, source_target_pairs={{0,16},{16,32},{32,48},{48,64},{64,80},{80,96},{96,112},{1,17},{17... | collective-permute-start | bytes 3145736 | tf_op jit(solution)/shard_map/ppermute | solution.py:20
  64.8 95.8 %copy-start.2 = (s32[8]{0:T(128)S(1)}, s32[8]{0:T(128)}, u32[]{:S(2)}) copy-start(s32[8]{0:T(128)} %param.11) | copy-start | bytes 100
  64.9 153.1 %all-gather.2.cloned.1.call-start = ((), (), s32[]{:S(2)}) async-start(), calls=%async_computation.2 | async-start | bytes 4456448 | tf_op jit(solution)/shard_map/all_gather | solution.py:145
Sparse Core Ops, SparseCore 0:
  65.0 93.7 reduce-scatter.1
  160.9 57.0 all-gather.1
